TPU v7x, 128 devices: a whole 4x4x4 slice. The times are simulated.
128 devices in a mesh: row: 8 (over z, core), col: 16 (over y, x).
Axes of the slice: x: 4, y: 4, z: 4, core: 2. Of those that a mesh axis runs over, the one named last changes fastest.
Arguments:
- u_factors: bfloat16 [16, 16, 192, 1024], P('row', 'col'), may hold values from -4 to 4
- v_factors: bfloat16 [16, 16, 192, 1024], P('row', 'col'), may hold values from -4 to 4
- diag_tiles: float32 [16, 1024, 1024], P('row', 'col'), as said below
- sketch: bfloat16 [192, 1024], replicated, may hold values from -1 to 1
- rank_levels: int32 [3, 16, 16], P(None, 'row', 'col'), may hold values from 64 to 192, as said below
Outputs:
- u_out: bfloat16 [16, 16, 192, 1024], P('row', 'col')
- v_out: bfloat16 [16, 16, 192, 1024], P('row', 'col')
- diag_out: float32 [16, 1024, 1024], P('row', 'col')
Inputs may be any that keep to these rules, and one draw needn't show every extreme that they name: Every entry is a multiple of 64; rank_levels[l + 1] <= rank_levels[l] entrywise; some tile (i, j) with i > j >= 2 has 192 at every level. `diag_tiles`: each tile is symmetric with eigenvalues between 2 and 20.
All inputs are finite; a program needn't handle non-finite values.
Results may differ from a plain program's by a relative error of at most 0.035.
Values may be sent and summed in bfloat16 or wider, within the bound.
No kernel may reach another device: no remote copies, remote signals or barrier semaphores. Data moves between devices by JAX's collectives and lax.ppermute only.
A program may use at most 128 MiB of HBM per device.

v0:
```python
import jax
import jax.numpy as jnp
from jax import lax
from jax.sharding import PartitionSpec as P

PANELS = 2


highest = lax.Precision.HIGHEST


def broadcast(shard, axis, root):
    mine = lax.axis_index(axis) == root
    return lax.psum(jnp.where(mine, shard, jnp.zeros_like(shard)), axis)


def chol_apply(factor, rhs):
    middle = jax.scipy.linalg.solve_triangular(factor, rhs, lower=True)
    return jax.scipy.linalg.solve_triangular(factor, middle, lower=True, trans=1)


def solve_panel(chol_k, raw_factors):
    tile_count, rank_width, tile_order = raw_factors.shape
    flattened = raw_factors.reshape(tile_count * rank_width, tile_order).astype(jnp.float32).T
    solved = jax.scipy.linalg.solve_triangular(chol_k, flattened, lower=True)
    return solved.T.reshape(tile_count, rank_width, tile_order).astype(jnp.bfloat16)


def factor_tile(tile_mat):
    return jnp.linalg.cholesky(tile_mat)


def zero_tile(tile_mat):
    return jnp.zeros_like(tile_mat)


def zero_factors(chol_k, raw_factors):
    return jnp.zeros_like(raw_factors)


def on_device(u_factors, v_factors, diag_tiles, sketch, rank_levels):
    row_count = lax.axis_size("row")
    col_count = lax.axis_size("col")
    row_index = lax.axis_index("row")
    col_index = lax.axis_index("col")
    tiles_row, tiles_col, rank_width, tile_order = u_factors.shape
    diag_rows = diag_tiles.shape[1]
    col_ratio = col_count // row_count
    row_tile = jnp.arange(tiles_row, dtype=jnp.int32) * row_count + row_index
    col_tile = jnp.arange(tiles_col, dtype=jnp.int32) * col_count + col_index
    rank_slots = jnp.arange(rank_width, dtype=jnp.int32)
    identity = jnp.eye(rank_width, dtype=jnp.float32)
    zero_bf = jnp.zeros((), jnp.bfloat16)
    below_diag = row_tile[:, None] > col_tile[None, :]
    live_rows = (rank_slots[None, None, :] < rank_levels[0][:, :, None]) & below_diag[:, :, None]
    factor_u = jnp.where(live_rows[..., None], u_factors, zero_bf)
    factor_v = jnp.where(live_rows[..., None], v_factors, zero_bf)
    diagonal = diag_tiles
    first_row = col_index * diag_rows
    pick_slot = col_index // row_count
    for panel_index in range(PANELS):
        diag_slot = panel_index // row_count
        diag_owner = panel_index % row_count
        col_slot = panel_index // col_count
        col_owner = panel_index % col_count
        whole_tile = lax.all_gather(diagonal[diag_slot], "col", axis=0, tiled=True)
        raw_u = factor_u[:, col_slot]
        raw_v = factor_v[:, col_slot]
        own_chol = lax.cond(row_index == diag_owner, factor_tile, zero_tile, whole_tile)
        chol_k = broadcast(own_chol, "row", diag_owner)
        sent_v = lax.cond(col_index == col_owner, solve_panel, zero_factors, chol_k, raw_v)
        row_u, row_second = (
            broadcast(raw_u, "col", col_owner),
            broadcast(sent_v, "col", col_owner),
        )
        relay_u = lax.dynamic_index_in_dim(
            row_u.reshape(tiles_col, col_ratio, rank_width, tile_order),
            pick_slot,
            1,
            keepdims=False,
        )
        relay_v = lax.dynamic_index_in_dim(
            row_second.reshape(tiles_col, col_ratio, rank_width, tile_order),
            pick_slot,
            1,
            keepdims=False,
        )
        col_u, col_second = (
            broadcast(relay_u, "row", col_index % row_count),
            broadcast(relay_v, "row", col_index % row_count),
        )
        row_v = row_second
        col_v = col_second
        row_live = (row_tile > panel_index)[:, None, None]
        col_live = (col_tile > panel_index)[:, None, None]
        row_u = jnp.where(row_live, row_u, zero_bf)
        row_v = jnp.where(row_live, row_v, zero_bf)
        col_u = jnp.where(col_live, col_u, zero_bf)
        col_v = jnp.where(col_live, col_v, zero_bf)
        coupling = jnp.einsum("arx,bsx->abrs", row_v, col_v, preferred_element_type=jnp.float32)
        col_sketch = jnp.einsum("rx,bsx->brs", sketch, col_u, preferred_element_type=jnp.float32)
        sketch_v = jnp.einsum(
            "rx,absx->abrs", sketch, factor_v, preferred_element_type=jnp.float32
        ).astype(jnp.bfloat16)
        sketch_c = jnp.einsum("brs,abts->abrt", col_sketch, coupling, precision=highest).astype(
            jnp.bfloat16
        )
        range_y = jnp.einsum(
            "abrs,absx->abrx", sketch_v, factor_u, preferred_element_type=jnp.float32
        )
        range_y = range_y - jnp.einsum(
            "abrs,asx->abrx", sketch_c, row_u, preferred_element_type=jnp.float32
        )
        keep_rows = rank_slots[None, None, :] < rank_levels[panel_index + 1][:, :, None]
        range_y = jnp.where(keep_rows[..., None], range_y, 0.0).astype(jnp.bfloat16)
        gram_matrix = jnp.einsum(
            "abrx,absx->abrs", range_y, range_y, preferred_element_type=jnp.float32
        )
        gram_matrix = gram_matrix + (1.0 - keep_rows.astype(jnp.float32))[..., None] * identity
        proj_u = jnp.einsum(
            "abrx,absx->abrs", range_y, factor_u, preferred_element_type=jnp.float32
        )
        proj_own = jnp.einsum("abrx,asx->abrs", range_y, row_u, preferred_element_type=jnp.float32)
        proj_c = jnp.einsum("abrs,abst->abrt", proj_own, coupling, precision=highest)
        gram_chol = jnp.linalg.cholesky(gram_matrix)
        first_core = chol_apply(gram_chol, proj_u).astype(jnp.bfloat16)
        second_core = chol_apply(gram_chol, proj_c).astype(jnp.bfloat16)
        fresh_v = jnp.einsum(
            "abrs,absx->abrx", first_core, factor_v, preferred_element_type=jnp.float32
        )
        fresh_v = (
            fresh_v
            - jnp.einsum("abrs,bsx->abrx", second_core, col_u, preferred_element_type=jnp.float32)
        ).astype(jnp.bfloat16)
        update_mask = ((row_tile[:, None] > col_tile[None, :]) & (col_tile[None, :] > panel_index))[
            ..., None, None
        ]
        at_panel = ((col_tile[None, :] == panel_index) & (row_tile[:, None] > panel_index))[
            ..., None, None
        ]
        factor_u = jnp.where(update_mask, range_y, jnp.where(at_panel, row_u[:, None], factor_u))
        factor_v = jnp.where(update_mask, fresh_v, jnp.where(at_panel, row_v[:, None], factor_v))
        self_c = jnp.einsum(
            "arx,asx->ars", row_v, row_v, preferred_element_type=jnp.float32
        ).astype(jnp.bfloat16)
        spread = jnp.einsum(
            "ars,asx->arx", self_c, row_u, preferred_element_type=jnp.float32
        ).astype(jnp.bfloat16)
        part_u = lax.dynamic_slice_in_dim(row_u, first_row, diag_rows, 2)
        lowered = diagonal - jnp.einsum(
            "arx,ary->axy", part_u, spread, preferred_element_type=jnp.float32
        )
        chol_rows = lax.dynamic_slice_in_dim(chol_k, first_row, diag_rows, 0)
        diag_tile = row_tile[:, None, None]
        diagonal = jnp.where(
            diag_tile > panel_index,
            lowered,
            jnp.where(diag_tile == panel_index, chol_rows[None], diagonal),
        )
    return (factor_u, factor_v, diagonal)


def solution(mesh):
    in_specs = (
        P("row", "col", None, None),
        P("row", "col", None, None),
        P("row", "col", None),
        P(),
        P(None, "row", "col"),
    )
    out_specs = (P("row", "col", None, None), P("row", "col", None, None), P("row", "col", None))
    return jax.shard_map(
        on_device, mesh=mesh, in_specs=in_specs, out_specs=out_specs, check_vma=False
    )
```

profile of v0, /device:TPU:37, one launch (start us, length us, event | category | flops | bytes accessed | tf_op | source)
XLA Modules:
  0.0 1576.1 jit_solution(8242127714323759272)
XLA Ops:
  9.3 54.5 %all-gather.5.cloned.1.call-done = f32[1,1024,1024]{2,0,1:T(1,128)} async-done(((f32[1,64,1024]{2,0,1:T(1,128)}), f32[1,1024,1024]{2,0,1:T(1,128)}) %all-gather.5.cloned.1.call-update) | async-done | bytes 4194320 | tf_op jit(solution)/shard_map/all_gather | solution.py:66
  63.8 11.0 conditional.4
  74.8 2.8 broadcast_select_fusion.1
  80.4 281.2 %all-reduce.17.cloned.1.call-done = f32[1024,1024]{1,0:T(8,128)} async-done(((f32[1024,1024]{1,0:T(8,128)}), f32[1024,1024]{1,0:T(8,128)}) %all-reduce.17.cloned.1.call-update) | async-done | bytes 4194320 | tf_op jit(solution)/shard_map/psum | solution.py:14
  363.7 208.2 %all-reduce.23.cloned.1.call-done = (bf16[2,192,1024]{2,1,0:T(8,128)(2,1)}, bf16[2,192,1024]{2,1,0:T(8,128)(2,1)}) async-done(((bf16[2,192,1024]{2,1,0:T(8,128)(2,1)}, bf16[2,192,1024]{2,1,0:T(8,128)(2,1)}), (bf16[2,192,1024]{2,1,0:T(8,128)(2,1)}, bf16[2,192,1024]{2,1,0:T(8,128)(2,1)})) %all-reduce.23.cloned.1.call-update) | async-done | bytes 1572880 | tf_op jit(solution)/shard_map/psum | solution.py:14
  575.4 10.3 all-gather.7.cloned.1.call-start
  597.9 2.9 fusion.138
  600.8 35.1 %all-reduce.27.cloned.1.call-done = (bf16[1,192,1024]{2,1,0:T(8,128)(2,1)}, bf16[1,192,1024]{2,1,0:T(8,128)(2,1)}) async-done(((bf16[1,192,1024]{2,1,0:T(8,128)(2,1)}, bf16[1,192,1024]{2,1,0:T(8,128)(2,1)}), (bf16[1,192,1024]{2,1,0:T(8,128)(2,1)}, bf16[1,192,1024]{2,1,0:T(8,128)(2,1)})) %all-reduce.27.cloned.1.call-update) | async-done | bytes 786448 | tf_op jit(solution)/shard_map/psum | solution.py:14
  648.0 24.9 %custom-call.96 = f32[2,1,128,128]{3,2,1,0:T(8,128)} custom-call(f32[2,1,128,128]{3,2,1,0:T(8,128)} %slice_bitcast_fusion.38), custom_call_target="Cholesky" | custom-call | tf_op jit(solution)/shard_map/jit(cholesky)/cholesky | solution.py:125
  675.1 21.1 %custom-call.97 = f32[2,1,1,128,128]{3,4,2,1,0:T(8,128)} custom-call(f32[2,1,1,128,128]{4,3,2,1,0:T(8,128)} %get-tuple-element.310), custom_call_target="InvertDiagBlocksLowerTriangular" | custom-call | tf_op jit(solution)/shard_map/jit(cholesky)/cholesky | solution.py:125
  701.4 13.1 custom-call.98
  722.1 40.7 %custom-call.100 = f32[2,2,128,128]{2,3,1,0:T(8,128)} custom-call(f32[2,2,128,128]{3,2,1,0:T(8,128)} %copy.344), custom_call_target="InvertDiagBlocksLowerTriangular" | custom-call | tf_op jit(solution)/shard_map/jit(_solve_triangular)/vmap()/triangular_solve | solution.py:19
  764.5 40.9 %custom-call.101 = f32[2,2,128,128]{2,3,1,0:T(8,128)} custom-call(f32[2,2,128,128]{3,2,1,0:T(8,128)} %pad_maximum_fusion.1), custom_call_target="InvertDiagBlocksLowerTriangular" | custom-call | tf_op jit(solution)/shard_map/jit(_solve_triangular)/vmap()/triangular_solve | solution.py:18
  815.6 6.3 conditional.6
  834.7 276.5 %all-reduce.19.cloned.1.call-done = f32[1024,1024]{1,0:T(8,128)} async-done(((f32[1024,1024]{1,0:T(8,128)}), f32[1024,1024]{1,0:T(8,128)}) %all-reduce.19.cloned.1.call-update) | async-done | bytes 4194320 | tf_op jit(solution)/shard_map/psum | solution.py:14
  1112.5 9.2 all-reduce.25.cloned.1.call-start
  1123.0 3.4 fusion.140
  1127.4 196.0 %all-reduce.21.cloned.1.call-done = (bf16[2,192,1024]{2,1,0:T(8,128)(2,1)}, bf16[2,192,1024]{2,1,0:T(8,128)(2,1)}) async-done(((bf16[2,192,1024]{2,1,0:T(8,128)(2,1)}, bf16[2,192,1024]{2,1,0:T(8,128)(2,1)}), (bf16[2,192,1024]{2,1,0:T(8,128)(2,1)}, bf16[2,192,1024]{2,1,0:T(8,128)(2,1)})) %all-reduce.21.cloned.1.call-update) | async-done | bytes 1572880 | tf_op jit(solution)/shard_map/psum | solution.py:14
  1331.4 57.4 %all-reduce.25.cloned.1.call-done = (bf16[1,192,1024]{2,1,0:T(8,128)(2,1)}, bf16[1,192,1024]{2,1,0:T(8,128)(2,1)}) async-done(((bf16[1,192,1024]{2,1,0:T(8,128)(2,1)}, bf16[1,192,1024]{2,1,0:T(8,128)(2,1)}), (bf16[1,192,1024]{2,1,0:T(8,128)(2,1)}, bf16[1,192,1024]{2,1,0:T(8,128)(2,1)})) %all-reduce.25.cloned.1.call-update) | async-done | bytes 786448 | tf_op jit(solution)/shard_map/psum | solution.py:14
  1397.4 23.5 %custom-call.103 = f32[2,1,128,128]{3,2,1,0:T(8,128)S(1)} custom-call(f32[2,1,128,128]{3,2,1,0:T(8,128)S(1)} %cholesky.1200), custom_call_target="Cholesky" | custom-call | tf_op jit(solution)/shard_map/jit(cholesky)/cholesky | solution.py:125
  1422.2 19.7 %custom-call.104 = f32[2,1,1,128,128]{3,4,2,1,0:T(8,128)S(1)} custom-call(f32[2,1,1,128,128]{4,3,2,1,0:T(8,128)S(1)} %get-tuple-element.308), custom_call_target="InvertDiagBlocksLowerTriangular" | custom-call | tf_op jit(solution)/shard_map/jit(cholesky)/cholesky | solution.py:125
  1444.0 11.7 custom-call.105
  1461.6 40.3 %custom-call.107 = f32[2,2,128,128]{2,3,1,0:T(8,128)S(1)} custom-call(f32[2,2,128,128]{3,2,1,0:T(8,128)} %copy.377), custom_call_target="InvertDiagBlocksLowerTriangular" | custom-call | tf_op jit(solution)/shard_map/jit(_solve_triangular)/vmap()/triangular_solve | solution.py:19
  1510.1 40.8 %custom-call.108 = f32[2,2,128,128]{2,3,1,0:T(8,128)} custom-call(f32[2,2,128,128]{3,2,1,0:T(8,128)} %pad_maximum_fusion.3), custom_call_target="InvertDiagBlocksLowerTriangular" | custom-call | tf_op jit(solution)/shard_map/jit(_solve_triangular)/vmap()/triangular_solve | solution.py:18
  (238 shorter events, 134.6 us)
Async XLA Ops:
  7.2 590.7 %copy-start = (bf16[192,1024]{1,0:T(8,128)(2,1)S(1)}, bf16[192,1024]{1,0:T(8,128)(2,1)}, u32[]{:S(2)}) copy-start(bf16[192,1024]{1,0:T(8,128)(2,1)} %param.24) | copy-start | bytes 1179652
  7.2 56.6 %all-gather.5.cloned.1.call-start = ((), (), s32[]{:S(2)}) async-start(), calls=%async_computation.2 | async-start | bytes 4456448 | tf_op jit(solution)/shard_map/all_gather | solution.py:66
  9.2 352.3 %all-reduce.17.cloned.1.call-start = ((), (), s32[]{:S(2)}) async-start(), calls=%async_computation | async-start | bytes 8388608 | tf_op jit(solution)/shard_map/psum | solution.py:14
  77.7 494.3 %all-reduce.23.cloned.1.call-start = ((), (), s32[]{:S(2)}) async-start(), calls=%async_computation.5 | async-start | bytes 3145728 | tf_op jit(solution)/shard_map/psum | solution.py:14
  79.3 282.3 %copy-start.36 = (pred[2,192]{1,0:T(4,128)(4,1)}, pred[2,192]{1,0:T(4,128)(4,1)S(1)}, u32[]{:S(2)}) copy-start(pred[2,192]{1,0:T(4,128)(4,1)S(1)} %compare_and_fusion) | copy-start | bytes 1156
  362.6 273.3 %all-reduce.27.cloned.1.call-start = ((), (), s32[]{:S(2)}) async-start(), calls=%async_computation.7 | async-start | bytes 1572864 | tf_op jit(solution)/shard_map/psum | solution.py:14
  362.7 227.2 %copy-start.43 = (pred[2]{0:T(512)(128)(4,1)}, pred[2]{0:T(512)(128)(4,1)S(1)}, u32[]{:S(2)}) copy-start(pred[2]{0:T(512)(128)(4,1)S(1)} %get-tuple-element.319) | copy-start | bytes 10
  573.2 24.7 %copy-start.11 = (bf16[2,1,192,1024]{3,2,1,0:T(8,128)(2,1)S(1)}, bf16[2,1,192,1024]{3,2,1,0:T(8,128)(2,1)}, u32[]{:S(2)}) copy-start(bf16[2,1,192,1024]{3,2,1,0:T(8,128)(2,1)} %param.21) | copy-start | bytes 2359300
  575.4 240.2 %all-gather.7.cloned.1.call-start = ((), (), s32[]{:S(2)}) async-start(), calls=%async_computation.3 | async-start | bytes 4456448 | tf_op jit(solution)/shard_map/all_gather | solution.py:66
  589.9 50.2 %copy-start.6 = (f32[2,64,1024]{2,1,0:T(8,128)}, f32[2,64,1024]{2,1,0:T(8,128)S(1)}, u32[]{:S(2)}) copy-start(f32[2,64,1024]{2,1,0:T(8,128)S(1)} %fusion.134) | copy-start | bytes 1572868
  590.7 46.7 %copy-start.44 = (pred[2]{0:T(512)(128)(4,1)S(1)}, pred[2]{0:T(512)(128)(4,1)}, u32[]{:S(2)}) copy-start(pred[2]{0:T(512)(128)(4,1)} %copy-done.43) | copy-start | bytes 10
  590.7 520.5 %all-reduce.19.cloned.1.call-start = ((), (), s32[]{:S(2)}) async-start(), calls=%async_computation.1 | async-start | bytes 8388608 | tf_op jit(solution)/shard_map/psum | solution.py:14
  824.7 8.6 copy-start.49
  824.7 8.6 copy-start.51
  824.8 498.7 %all-reduce.21.cloned.1.call-start = ((), (), s32[]{:S(2)}) async-start(), calls=%async_computation.4 | async-start | bytes 3145728 | tf_op jit(solution)/shard_map/psum | solution.py:14
  1112.5 276.3 %all-reduce.25.cloned.1.call-start = ((), (), s32[]{:S(2)}) async-start(), calls=%async_computation.6 | async-start | bytes 1572864 | tf_op jit(solution)/shard_map/psum | solution.py:14
  1122.3 266.5 %copy-start.40 = (pred[2]{0:T(512)(128)(4,1)}, pred[2]{0:T(512)(128)(4,1)S(1)}, u32[]{:S(2)}) copy-start(pred[2]{0:T(512)(128)(4,1)S(1)} %get-tuple-element.317) | copy-start | bytes 10
  1126.4 203.7 %copy-start.7 = (f32[2,64,1024]{2,1,0:T(8,128)S(1)}, f32[2,64,1024]{2,1,0:T(8,128)}, u32[]{:S(2)}) copy-start(f32[2,64,1024]{2,1,0:T(8,128)} %copy-done.6) | copy-start | bytes 1572868
  1458.4 93.9 %copy-start.14 = (f32[2,192,192]{2,1,0:T(8,128)}, f32[2,192,192]{2,1,0:T(8,128)S(1)}, u32[]{:S(2)}) copy-start(f32[2,192,192]{2,1,0:T(8,128)S(1)} %bitcast_select_fusion.10) | copy-start | bytes 884740
  1508.3 58.4 %copy-start.5 = (bf16[2,192,1024]{2,1,0:T(8,128)(2,1)S(1)}, bf16[2,192,1024]{2,1,0:T(8,128)(2,1)}, u32[]{:S(2)}) copy-start(bf16[2,192,1024]{2,1,0:T(8,128)(2,1)} %get-tuple-element.173) | copy-start | bytes 2359300
  1508.3 58.4 %copy-start.41 = (pred[2]{0:T(512)(128)(4,1)S(1)}, pred[2]{0:T(512)(128)(4,1)}, u32[]{:S(2)}) copy-start(pred[2]{0:T(512)(128)(4,1)} %copy-done.40) | copy-start | bytes 10
  1508.3 58.4 %copy-start.46 = (pred[2]{0:T(512)(128)(4,1)S(1)}, pred[2]{0:T(512)(128)(4,1)}, u32[]{:S(2)}) copy-start(pred[2]{0:T(512)(128)(4,1)} %get-tuple-element.181) | copy-start | bytes 10
  1508.3 58.4 %copy-start.47 = (pred[2]{0:T(512)(128)(4,1)S(1)}, pred[2]{0:T(512)(128)(4,1)}, u32[]{:S(2)}) copy-start(pred[2]{0:T(512)(128)(4,1)} %broadcast_and_fusion) | copy-start | bytes 10
  1553.9 13.9 copy-start.8
  (31 other events, 106.1 us)
Sparse Core Ops, SparseCore 0:
  10.7 53.0 all-gather.4
  77.8 283.7 all-reduce.16
  365.5 206.4 all-reduce.22
  575.5 60.3 all-reduce.26
  637.9 54.5 all-gather.6
  824.9 286.3 all-reduce.18
  1115.2 208.2 all-reduce.20
  1328.4 60.3 all-reduce.24
where the time goes:
time: 1590 us; the launch traced here: 1580 us
  waiting for transfers between devices  1110 us (70%)
  other arithmetic  320 us (20%)
  matrix products  72.6 us (5%)
  local copies, waits for them, and re-layouts  27.2 us (2%)
  starting transfers between devices  19.8 us (1%)
    psum x6, waiting for transfers between devices, broadcast(): return lax.psum(jnp.where(mine, shard, jnp.zeros_like(shard)), axis)  1050 us
    another operation x18, other arithmetic, on_device(): gram_chol = jnp.linalg.cholesky(gram_matrix)  122 us
    another operation x11, other arithmetic, chol_apply(): jax.scipy.linalg.solve_triangular(factor, middle, lower=True, trans=1)  87 us
    another operation x4, other arithmetic, chol_apply(): middle = jax.scipy.linalg.solve_triangular(factor, rhs, lower=True)  85.2 us
    all_gather x2, waiting for transfers between devices, on_device(): whole_tile = lax.all_gather(diagonal[diag_slot], 'col', axis=0, tiled=True)  54.5 us
  transfers between devices with their start and end apart: 8, of which 7 were waited for; matrix products, arithmetic and copies ran while one was open for 14% of the time, Pallas kernels for 0%

commit v1 on v0

--- a/solution.py
+++ b/solution.py
@@ -63,15 +63,11 @@
         diag_owner = panel_index % row_count
         col_slot = panel_index // col_count
         col_owner = panel_index % col_count
-        whole_tile = lax.all_gather(diagonal[diag_slot], "col", axis=0, tiled=True)
         raw_u = factor_u[:, col_slot]
         raw_v = factor_v[:, col_slot]
-        own_chol = lax.cond(row_index == diag_owner, factor_tile, zero_tile, whole_tile)
-        chol_k = broadcast(own_chol, "row", diag_owner)
-        sent_v = lax.cond(col_index == col_owner, solve_panel, zero_factors, chol_k, raw_v)
-        row_u, row_second = (
+        row_u, row_raw = (
             broadcast(raw_u, "col", col_owner),
-            broadcast(sent_v, "col", col_owner),
+            broadcast(raw_v, "col", col_owner),
         )
         relay_u = lax.dynamic_index_in_dim(
             row_u.reshape(tiles_col, col_ratio, rank_width, tile_order),
@@ -80,17 +76,21 @@
             keepdims=False,
         )
         relay_v = lax.dynamic_index_in_dim(
-            row_second.reshape(tiles_col, col_ratio, rank_width, tile_order),
+            row_raw.reshape(tiles_col, col_ratio, rank_width, tile_order),
             pick_slot,
             1,
             keepdims=False,
         )
-        col_u, col_second = (
+        col_u, col_raw = (
             broadcast(relay_u, "row", col_index % row_count),
             broadcast(relay_v, "row", col_index % row_count),
         )
-        row_v = row_second
-        col_v = col_second
+        whole_tile = lax.all_gather(diagonal[diag_slot], "col", axis=0, tiled=True)
+        own_chol = lax.cond(row_index == diag_owner, factor_tile, zero_tile, whole_tile)
+        chol_k = broadcast(own_chol, "row", diag_owner)
+        solved = solve_panel(chol_k, jnp.concatenate([row_raw, col_raw], axis=0))
+        row_v = solved[:tiles_row]
+        col_v = solved[tiles_row:]
         row_live = (row_tile > panel_index)[:, None, None]
         col_live = (col_tile > panel_index)[:, None, None]
         row_u = jnp.where(row_live, row_u, zero_bf)
@@ -123,8 +123,14 @@
         proj_own = jnp.einsum("abrx,asx->abrs", range_y, row_u, preferred_element_type=jnp.float32)
         proj_c = jnp.einsum("abrs,abst->abrt", proj_own, coupling, precision=highest)
         gram_chol = jnp.linalg.cholesky(gram_matrix)
-        first_core = chol_apply(gram_chol, proj_u).astype(jnp.bfloat16)
-        second_core = chol_apply(gram_chol, proj_c).astype(jnp.bfloat16)
+        gram_inv = jax.scipy.linalg.solve_triangular(
+            gram_chol, jnp.broadcast_to(identity, gram_chol.shape), lower=True
+        )
+        both = jnp.concatenate([proj_u, proj_c], axis=-1)
+        middle = jnp.einsum("abrs,abst->abrt", gram_inv, both, precision=highest)
+        cores = jnp.einsum("absr,abst->abrt", gram_inv, middle, precision=highest)
+        first_core = cores[..., :rank_width].astype(jnp.bfloat16)
+        second_core = cores[..., rank_width:].astype(jnp.bfloat16)
         fresh_v = jnp.einsum(
             "abrs,absx->abrx", first_core, factor_v, preferred_element_type=jnp.float32
         )

time: 1590 us -> 1430 us (0.90)
  waiting for transfers between devices: 1110 us -> 827 us
  other arithmetic: 320 us -> 400 us
  local copies, waits for them, and re-layouts: 27.2 us -> 78.8 us
  starting transfers between devices: 19.8 us -> 0.33 us
    psum x6, waiting for transfers between devices: 1050 us -> 721 us  [broadcast(): return lax.psum(jnp.where(mine, shard, jnp.zeros_like(shard)), axis)]
    another operation x15 -> x16, other arithmetic: 172 us -> 254 us  [the longest x5 170 us: solve_panel(): solved = jax.scipy.linalg.solve_triangular(chol_k, flattened, lower=True)]
    another operation x15 -> x60, local copies, waits for them, and re-layouts: 11.6 us -> 63.7 us  [the longest x51 57.7 us: solve_panel(): solved = jax.scipy.linalg.solve_triangular(chol_k, flattened, lower=True)]
    all_gather x2, waiting for transfers between devices: 54.5 us -> 106 us  [on_device(): whole_tile = lax.all_gather(diagonal[diag_slot], 'col', axis=0, tiled=True)]
    another operation x24 -> x36, matrix products: 28.3 us -> 44.9 us  [the longest x30 38.2 us: solve_panel(): solved = jax.scipy.linalg.solve_triangular(chol_k, flattened, lower=True)]
  transfers between devices with their start and end apart: 8 -> 8, of which waited for: 7 -> 8; matrix products, arithmetic and copies ran while one was open for 14% -> 3% of each run, Pallas kernels for 0% -> 0%
where the time goes in v1:
time: 1430 us; the launch traced here: 1420 us
  waiting for transfers between devices  827 us (58%)
  other arithmetic  400 us (28%)
  matrix products  87.8 us (6%)
  local copies, waits for them, and re-layouts  78.8 us (6%)
  between operations  15.7 us (1%)
    psum x6, waiting for transfers between devices, broadcast(): return lax.psum(jnp.where(mine, shard, jnp.zeros_like(shard)), axis)  721 us
    another operation x5, other arithmetic, solve_panel(): solved = jax.scipy.linalg.solve_triangular(chol_k, flattened, lower=True)  170 us
    another operation x18, other arithmetic, on_device(): gram_chol = jnp.linalg.cholesky(gram_matrix)  119 us
    all_gather x2, waiting for transfers between devices, on_device(): whole_tile = lax.all_gather(diagonal[diag_slot], 'col', axis=0, tiled=True)  106 us
    another operation x11, other arithmetic, on_device(): jax.scipy.linalg.solve_triangular(gram_chol, jnp.broadcast_to(identity, g...  84.2 us
    another operation x51, local copies, waits for them, and re-layouts, solve_panel(): solved = jax.scipy.linalg.solve_triangular(chol_k, flattened, lower=True)  57.7 us
    another operation x30, matrix products, solve_panel(): solved = jax.scipy.linalg.solve_triangular(chol_k, flattened, lower=True)  38.2 us
  transfers between devices with their start and end apart: 8, of which 8 were waited for; matrix products, arithmetic and copies ran while one was open for 3% of the time, Pallas kernels for 0%

profile of v1, /device:TPU:37, one launch (start us, length us, event | category | flops | bytes accessed | tf_op | source)
XLA Modules:
  0.0 1418.1 jit_solution(11081613754306571204)
XLA Ops:
  14.7 85.3 %all-reduce.21.cloned.1.call-done = (bf16[2,192,1024]{2,1,0:T(8,128)(2,1)}, bf16[2,192,1024]{2,1,0:T(8,128)(2,1)}) async-done(((bf16[2,192,1024]{2,1,0:T(8,128)(2,1)}, bf16[2,192,1024]{2,1,0:T(8,128)(2,1)}), (bf16[2,192,1024]{2,1,0:T(8,128)(2,1)}, bf16[2,192,1024]{2,1,0:T(8,128)(2,1)})) %all-reduce.21.cloned.1.call-update) | async-done | bytes 1572880 | tf_op jit(solution)/shard_map/psum | solution.py:14
  102.1 53.4 %all-gather.5.cloned.1.call-done = f32[1,1024,1024]{2,0,1:T(1,128)} async-done(((f32[1,64,1024]{2,0,1:T(1,128)}), f32[1,1024,1024]{2,0,1:T(1,128)}) %all-gather.5.cloned.1.call-update) | async-done | bytes 4194320 | tf_op jit(solution)/shard_map/all_gather | solution.py:88
  155.5 6.9 conditional.2
  174.2 42.5 %all-reduce.25.cloned.1.call-done = (bf16[1,192,1024]{2,1,0:T(8,128)(2,1)}, bf16[1,192,1024]{2,1,0:T(8,128)(2,1)}) async-done(((bf16[1,192,1024]{2,1,0:T(8,128)(2,1)}, bf16[1,192,1024]{2,1,0:T(8,128)(2,1)}), (bf16[1,192,1024]{2,1,0:T(8,128)(2,1)}, bf16[1,192,1024]{2,1,0:T(8,128)(2,1)})) %all-reduce.25.cloned.1.call-update) | async-done | bytes 786448 | tf_op jit(solution)/shard_map/psum | solution.py:14
  219.1 234.9 %all-reduce.15.cloned.1.call-done = f32[1024,1024]{1,0:T(8,128)} async-done(((f32[1024,1024]{1,0:T(8,128)}), f32[1024,1024]{1,0:T(8,128)}) %all-reduce.15.cloned.1.call-update) | async-done | bytes 4194320 | tf_op jit(solution)/shard_map/psum | solution.py:14
  454.0 4.8 fusion.57
  460.2 33.3 %while.7 = (s32[]{:T(128)}, f32[1024,1024]{1,0:T(8,128)}, s32[8,2]{0,1:T(2,128)}, f32[8,128,128]{2,1,0:T(8,128)}, s32[]{:T(128)}) while((s32[]{:T(128)}, f32[1024,1024]{1,0:T(8,128)}, s32[8,2]{0,1:T(2,128)}, f32[8,128,128]{2,1,0:T(8,128)}, s32[]{:T(128)}) %tuple.166), condition=%wide.while_cond, body=%wide.while_body.sunk | while | flops 2 | bytes 132205 | solution.py:25
  493.4 80.2 %custom-call.86 = f32[8,128,128]{1,2,0:T(8,128)} custom-call(f32[8,128,128]{2,1,0:T(8,128)} %get-tuple-element.55), custom_call_target="InvertDiagBlocksLowerTriangular" | custom-call | tf_op jit(solution)/shard_map/jit(_solve_triangular)/triangular_solve | solution.py:25
  599.8 23.5 %custom-call.87 = f32[2,1,128,128]{3,2,1,0:T(8,128)S(1)} custom-call(f32[2,1,128,128]{3,2,1,0:T(8,128)S(1)} %slice_bitcast_fusion.14), custom_call_target="Cholesky" | custom-call | tf_op jit(solution)/shard_map/jit(cholesky)/cholesky | solution.py:125
  623.4 20.3 %custom-call.88 = f32[2,1,1,128,128]{3,4,2,1,0:T(8,128)} custom-call(f32[2,1,1,128,128]{4,3,2,1,0:T(8,128)S(1)} %get-tuple-element.213), custom_call_target="InvertDiagBlocksLowerTriangular" | custom-call | tf_op jit(solution)/shard_map/jit(cholesky)/cholesky | solution.py:125
  646.1 11.7 custom-call.89
  659.8 39.7 %custom-call.90 = f32[2,2,128,128]{2,3,1,0:T(8,128)S(1)} custom-call(f32[2,2,128,128]{3,2,1,0:T(8,128)S(1)} %pad_maximum_fusion.8), custom_call_target="InvertDiagBlocksLowerTriangular" | custom-call | tf_op jit(solution)/shard_map/jit(_solve_triangular)/vmap()/triangular_solve | solution.py:126
  712.8 85.2 %all-reduce.19.cloned.1.call-done = (bf16[2,192,1024]{2,1,0:T(8,128)(2,1)}, bf16[2,192,1024]{2,1,0:T(8,128)(2,1)}) async-done(((bf16[2,192,1024]{2,1,0:T(8,128)(2,1)}, bf16[2,192,1024]{2,1,0:T(8,128)(2,1)}), (bf16[2,192,1024]{2,1,0:T(8,128)(2,1)}, bf16[2,192,1024]{2,1,0:T(8,128)(2,1)})) %all-reduce.19.cloned.1.call-update) | async-done | bytes 1572880 | tf_op jit(solution)/shard_map/psum | solution.py:14
  801.6 52.3 %all-gather.7.cloned.1.call-done = f32[1,1024,1024]{2,1,0:T(8,128)} async-done(((f32[1,64,1024]{2,1,0:T(8,128)}), f32[1,1024,1024]{2,1,0:T(8,128)}) %all-gather.7.cloned.1.call-update) | async-done | bytes 4194320 | tf_op jit(solution)/shard_map/all_gather | solution.py:88
  853.9 6.4 conditional.3
  868.6 46.4 %all-reduce.23.cloned.1.call-done = (bf16[1,192,1024]{2,1,0:T(8,128)(2,1)}, bf16[1,192,1024]{2,1,0:T(8,128)(2,1)}) async-done(((bf16[1,192,1024]{2,1,0:T(8,128)(2,1)}, bf16[1,192,1024]{2,1,0:T(8,128)(2,1)}), (bf16[1,192,1024]{2,1,0:T(8,128)(2,1)}, bf16[1,192,1024]{2,1,0:T(8,128)(2,1)})) %all-reduce.23.cloned.1.call-update) | async-done | bytes 786448 | tf_op jit(solution)/shard_map/psum | solution.py:14
  918.2 227.2 %all-reduce.17.cloned.1.call-done = f32[1024,1024]{1,0:T(8,128)} async-done(((f32[1024,1024]{1,0:T(8,128)}), f32[1024,1024]{1,0:T(8,128)}) %all-reduce.17.cloned.1.call-update) | async-done | bytes 4194320 | tf_op jit(solution)/shard_map/psum | solution.py:14
  1145.4 4.7 fusion.56
  1150.2 23.2 %while.8 = (s32[]{:T(128)}, f32[1024,1024]{1,0:T(8,128)}, s32[8,2]{0,1:T(2,128)S(1)}, f32[8,128,128]{2,1,0:T(8,128)S(1)}, s32[]{:T(128)}) while((s32[]{:T(128)}, f32[1024,1024]{1,0:T(8,128)}, s32[8,2]{0,1:T(2,128)S(1)}, f32[8,128,128]{2,1,0:T(8,128)S(1)}, s32[]{:T(128)}) %tuple.196), condition=%wide.while_cond.clone, body=%wide.while_body.clone.sunk | while | flops 2 | bytes 131189 | solution.py:25
  1173.4 79.6 %custom-call.91 = f32[8,128,128]{1,2,0:T(8,128)} custom-call(f32[8,128,128]{2,1,0:T(8,128)S(1)} %get-tuple-element.56), custom_call_target="InvertDiagBlocksLowerTriangular" | custom-call | tf_op jit(solution)/shard_map/jit(_solve_triangular)/triangular_solve | solution.py:25
  1284.5 24.9 %custom-call.92 = f32[2,1,128,128]{3,2,1,0:T(8,128)} custom-call(f32[2,1,128,128]{3,2,1,0:T(8,128)} %cholesky.1200), custom_call_target="Cholesky" | custom-call | tf_op jit(solution)/shard_map/jit(cholesky)/cholesky | solution.py:125
  1311.1 21.1 %custom-call.93 = f32[2,1,1,128,128]{3,4,2,1,0:T(8,128)} custom-call(f32[2,1,1,128,128]{4,3,2,1,0:T(8,128)} %get-tuple-element.211), custom_call_target="InvertDiagBlocksLowerTriangular" | custom-call | tf_op jit(solution)/shard_map/jit(cholesky)/cholesky | solution.py:125
  1337.4 13.1 custom-call.94
  1357.6 40.9 %custom-call.95 = f32[2,2,128,128]{2,3,1,0:T(8,128)} custom-call(f32[2,2,128,128]{3,2,1,0:T(8,128)} %pad_maximum_fusion.9), custom_call_target="InvertDiagBlocksLowerTriangular" | custom-call | tf_op jit(solution)/shard_map/jit(_solve_triangular)/vmap()/triangular_solve | solution.py:126
  (346 shorter events, 202.4 us)
Async XLA Ops:
  7.2 163.3 %copy-start = (bf16[192,1024]{1,0:T(8,128)(2,1)S(1)}, bf16[192,1024]{1,0:T(8,128)(2,1)}, u32[]{:S(2)}) copy-start(bf16[192,1024]{1,0:T(8,128)(2,1)} %param.18) | copy-start | bytes 1179652
  7.2 92.8 %all-reduce.21.cloned.1.call-start = ((), (), s32[]{:S(2)}) async-start(), calls=%async_computation.5 | async-start | bytes 3145728 | tf_op jit(solution)/shard_map/psum | solution.py:14
  8.3 161.6 %copy-start.56 = (s32[2]{0:T(128)}, s32[2]{0:T(128)S(1)}, u32[]{:S(2)}) copy-start(s32[2]{0:T(128)S(1)} %get-tuple-element.73) | copy-start | bytes 28
  8.9 161.6 %copy-start.52 = (pred[2,192]{1,0:T(4,128)(4,1)}, pred[2,192]{1,0:T(4,128)(4,1)S(1)}, u32[]{:S(2)}) copy-start(pred[2,192]{1,0:T(4,128)(4,1)S(1)} %compare_and_fusion) | copy-start | bytes 1156
  11.7 143.8 %all-gather.5.cloned.1.call-start = ((), (), s32[]{:S(2)}) async-start(), calls=%async_computation.2 | async-start | bytes 4456448 | tf_op jit(solution)/shard_map/all_gather | solution.py:88
  12.7 203.9 %all-reduce.25.cloned.1.call-start = ((), (), s32[]{:S(2)}) async-start(), calls=%async_computation.7 | async-start | bytes 1572864 | tf_op jit(solution)/shard_map/psum | solution.py:14
  14.7 151.2 %copy-start.8 = (f32[192,192]{0,1:T(8,128)}, f32[192,192]{0,1:T(8,128)S(1)}, u32[]{:S(2)}) copy-start(f32[192,192]{0,1:T(8,128)S(1)} %fusion.179) | copy-start | bytes 442372
  102.0 352.0 %all-reduce.15.cloned.1.call-start = ((), (), s32[]{:S(2)}) async-start(), calls=%async_computation | async-start | bytes 8388608 | tf_op jit(solution)/shard_map/psum | solution.py:14
  165.2 8.8 copy-start.11
  165.2 632.7 %all-reduce.19.cloned.1.call-start = ((), (), s32[]{:S(2)}) async-start(), calls=%async_computation.4 | async-start | bytes 3145728 | tf_op jit(solution)/shard_map/psum | solution.py:14
  170.5 46.2 %copy-start.12 = (bf16[2,192,1024]{2,1,0:T(8,128)(2,1)S(1)}, bf16[2,192,1024]{2,1,0:T(8,128)(2,1)}, u32[]{:S(2)}) copy-start(bf16[2,192,1024]{2,1,0:T(8,128)(2,1)} %get-tuple-element.95) | copy-start | bytes 2359300
  598.4 24.9 %copy-start.42 = (pred[128,128]{1,0:T(8,128)(4,1)S(1)}, pred[128,128]{1,0:T(8,128)(4,1)}, u32[]{:S(2)}) copy-start(pred[128,128]{1,0:T(8,128)(4,1)} %get-tuple-element.236) | copy-start | bytes 49156
  598.8 59.0 %copy-start.44 = (pred[64,64]{1,0:T(8,128)(4,1)S(1)}, pred[64,64]{1,0:T(8,128)(4,1)}, u32[]{:S(2)}) copy-start(pred[64,64]{1,0:T(8,128)(4,1)} %iota_compare_fusion.13) | copy-start | bytes 12292
  598.8 59.2 %copy-start.16 = (pred[192,192]{1,0:T(8,128)(4,1)S(1)}, pred[192,192]{1,0:T(8,128)(4,1)}, u32[]{:S(2)}) copy-start(pred[192,192]{1,0:T(8,128)(4,1)} %iota_compare_fusion.7) | copy-start | bytes 110596
  599.8 58.4 %copy-start.15 = (f32[2,192,192]{2,1,0:T(8,128)S(1)}, f32[2,192,192]{2,1,0:T(8,128)}, u32[]{:S(2)}) copy-start(f32[2,192,192]{2,1,0:T(8,128)} %fusion.237) | copy-start | bytes 884740
  643.7 55.9 %copy-start.17 = (f32[128,192]{1,0:T(8,128)S(1)}, f32[128,192]{1,0:T(8,128)}, u32[]{:S(2)}) copy-start(f32[128,192]{1,0:T(8,128)} %copy.268) | copy-start | bytes 294916
  643.7 56.4 %copy-start.34 = (f32[64,192]{1,0:T(8,128)S(1)}, f32[64,192]{1,0:T(8,128)}, u32[]{:S(2)}) copy-start(f32[64,192]{1,0:T(8,128)} %copy.269) | copy-start | bytes 147460
  659.7 45.4 %copy-start.18 = (f32[2,128,64]{2,1,0:T(8,128)}, f32[2,128,64]{2,1,0:T(8,128)S(1)}, u32[]{:S(2)}) copy-start(f32[2,128,64]{2,1,0:T(8,128)S(1)} %triangular_solve.386) | copy-start | bytes 196612
  708.5 145.4 %all-gather.7.cloned.1.call-start = ((), (), s32[]{:S(2)}) async-start(), calls=%async_computation.3 | async-start | bytes 4456448 | tf_op jit(solution)/shard_map/all_gather | solution.py:88
  711.9 142.0 %copy-start.6 = (f32[2,64,1024]{2,1,0:T(8,128)}, f32[2,64,1024]{2,1,0:T(8,128)S(1)}, u32[]{:S(2)}) copy-start(f32[2,64,1024]{2,1,0:T(8,128)S(1)} %fusion.68) | copy-start | bytes 1572868
  712.8 202.2 %all-reduce.23.cloned.1.call-start = ((), (), s32[]{:S(2)}) async-start(), calls=%async_computation.6 | async-start | bytes 1572864 | tf_op jit(solution)/shard_map/psum | solution.py:14
  801.5 343.9 %all-reduce.17.cloned.1.call-start = ((), (), s32[]{:S(2)}) async-start(), calls=%async_computation.1 | async-start | bytes 8388608 | tf_op jit(solution)/shard_map/psum | solution.py:14
  865.5 49.5 %copy-start.13 = (bf16[2,192,1024]{2,1,0:T(8,128)(2,1)S(1)}, bf16[2,192,1024]{2,1,0:T(8,128)(2,1)}, u32[]{:S(2)}) copy-start(bf16[2,192,1024]{2,1,0:T(8,128)(2,1)} %get-tuple-element.93) | copy-start | bytes 2359300
  918.2 232.0 %copy-start.43 = (s32[8,2]{0,1:T(2,128)S(1)}, s32[8,2]{0,1:T(2,128)}, u32[]{:S(2)}) copy-start(s32[8,2]{0,1:T(2,128)} %get-tuple-element.387) | copy-start | bytes 196
  (51 other events, 146.7 us)
Sparse Core Ops, SparseCore 0:
  11.9 87.9 all-reduce.20
  102.1 53.3 all-gather.4
  158.4 58.1 all-reduce.24
  218.9 235.0 all-reduce.14
  708.6 89.3 all-reduce.18
  800.5 53.3 all-gather.6
  856.9 58.0 all-reduce.22
  917.3 228.0 all-reduce.16

commit v2 on v1

--- a/solution.py
+++ b/solution.py
@@ -26,8 +26,45 @@
     return solved.T.reshape(tile_count, rank_width, tile_order).astype(jnp.bfloat16)
 
 
+BLOCK = 128
+
+
 def factor_tile(tile_mat):
-    return jnp.linalg.cholesky(tile_mat)
+    order = tile_mat.shape[0]
+    width = min(BLOCK, order)
+    count = order // width
+    work = (tile_mat + tile_mat.T) * 0.5
+    eye = jnp.eye(width, dtype=jnp.float32)
+    strips = []
+    for step in range(count):
+        head = jnp.tril(lax.linalg.cholesky(work[:width, :width], symmetrize_input=False))
+        head_inv = lax.linalg.triangular_solve(head, eye, left_side=True, lower=True)
+        parts = [jnp.zeros((step * width, width), jnp.float32), head + jnp.triu(head_inv.T, 1)]
+        if step < count - 1:
+            below = jnp.dot(work[width:, :width], head_inv.T, precision=highest)
+            work = work[width:, width:] - jnp.dot(below, below.T, precision=highest)
+            parts.append(below)
+        strips.append(jnp.concatenate(parts, axis=0))
+    return jnp.concatenate(strips, axis=1)
+
+
+def solve_packed(packed, raw_factors):
+    order = packed.shape[0]
+    width = min(BLOCK, order)
+    count = order // width
+    lead = raw_factors.shape[:-1]
+    rows = raw_factors.reshape(-1, order).astype(jnp.float32)
+    done = []
+    for step in range(count):
+        lo, hi = step * width, (step + 1) * width
+        block = packed[lo:hi, lo:hi]
+        inverse = jnp.tril(block.T, -1) + jnp.diag(1.0 / jnp.diagonal(block))
+        rhs = rows[:, lo:hi]
+        if step:
+            prior = jnp.concatenate(done, axis=1)
+            rhs = rhs - jnp.dot(prior, packed[lo:hi, :lo].T, precision=highest)
+        done.append(jnp.dot(rhs, inverse.T, precision=highest))
+    return jnp.concatenate(done, axis=1).reshape(lead + (order,)).astype(jnp.bfloat16)
 
 
 def zero_tile(tile_mat):
@@ -58,6 +95,9 @@
     diagonal = diag_tiles
     first_row = col_index * diag_rows
     pick_slot = col_index // row_count
+    chol_cols = jnp.arange(tile_order, dtype=jnp.int32)[None, :]
+    chol_rows_at = first_row + jnp.arange(diag_rows, dtype=jnp.int32)[:, None]
+    whole_tile = None
     for panel_index in range(PANELS):
         diag_slot = panel_index // row_count
         diag_owner = panel_index % row_count
@@ -65,6 +105,9 @@
         col_owner = panel_index % col_count
         raw_u = factor_u[:, col_slot]
         raw_v = factor_v[:, col_slot]
+        if whole_tile is None:
+            whole_tile = lax.all_gather(diagonal[diag_slot], "col", axis=0, tiled=True)
+            whole_tile, raw_u, raw_v = lax.optimization_barrier((whole_tile, raw_u, raw_v))
         row_u, row_raw = (
             broadcast(raw_u, "col", col_owner),
             broadcast(raw_v, "col", col_owner),
@@ -85,10 +128,10 @@
             broadcast(relay_u, "row", col_index % row_count),
             broadcast(relay_v, "row", col_index % row_count),
         )
-        whole_tile = lax.all_gather(diagonal[diag_slot], "col", axis=0, tiled=True)
         own_chol = lax.cond(row_index == diag_owner, factor_tile, zero_tile, whole_tile)
+        whole_tile = None
         chol_k = broadcast(own_chol, "row", diag_owner)
-        solved = solve_panel(chol_k, jnp.concatenate([row_raw, col_raw], axis=0))
+        solved = solve_packed(chol_k, jnp.concatenate([row_raw, col_raw], axis=0))
         row_v = solved[:tiles_row]
         col_v = solved[tiles_row:]
         row_live = (row_tile > panel_index)[:, None, None]
@@ -97,6 +140,27 @@
         row_v = jnp.where(row_live, row_v, zero_bf)
         col_u = jnp.where(col_live, col_u, zero_bf)
         col_v = jnp.where(col_live, col_v, zero_bf)
+        self_c = jnp.einsum(
+            "arx,asx->ars", row_v, row_v, preferred_element_type=jnp.float32
+        ).astype(jnp.bfloat16)
+        spread = jnp.einsum(
+            "ars,asx->arx", self_c, row_u, preferred_element_type=jnp.float32
+        ).astype(jnp.bfloat16)
+        part_u = lax.dynamic_slice_in_dim(row_u, first_row, diag_rows, 2)
+        lowered = diagonal - jnp.einsum(
+            "arx,ary->axy", part_u, spread, preferred_element_type=jnp.float32
+        )
+        chol_rows = lax.dynamic_slice_in_dim(chol_k, first_row, diag_rows, 0)
+        chol_rows = jnp.where(chol_cols <= chol_rows_at, chol_rows, 0.0)
+        diag_tile = row_tile[:, None, None]
+        diagonal = jnp.where(
+            diag_tile > panel_index,
+            lowered,
+            jnp.where(diag_tile == panel_index, chol_rows[None], diagonal),
+        )
+        if panel_index + 1 < PANELS:
+            next_slot = (panel_index + 1) // row_count
+            whole_tile = lax.all_gather(diagonal[next_slot], "col", axis=0, tiled=True)
         coupling = jnp.einsum("arx,bsx->abrs", row_v, col_v, preferred_element_type=jnp.float32)
         col_sketch = jnp.einsum("rx,bsx->brs", sketch, col_u, preferred_element_type=jnp.float32)
         sketch_v = jnp.einsum(
@@ -117,6 +181,8 @@
             "abrx,absx->abrs", range_y, range_y, preferred_element_type=jnp.float32
         )
         gram_matrix = gram_matrix + (1.0 - keep_rows.astype(jnp.float32))[..., None] * identity
+        if whole_tile is not None:
+            whole_tile, gram_matrix = lax.optimization_barrier((whole_tile, gram_matrix))
         proj_u = jnp.einsum(
             "abrx,absx->abrs", range_y, factor_u, preferred_element_type=jnp.float32
         )
@@ -138,6 +204,8 @@
             fresh_v
             - jnp.einsum("abrs,bsx->abrx", second_core, col_u, preferred_element_type=jnp.float32)
         ).astype(jnp.bfloat16)
+        if whole_tile is not None:
+            whole_tile, fresh_v = lax.optimization_barrier((whole_tile, fresh_v))
         update_mask = ((row_tile[:, None] > col_tile[None, :]) & (col_tile[None, :] > panel_index))[
             ..., None, None
         ]
@@ -146,23 +214,6 @@
         ]
         factor_u = jnp.where(update_mask, range_y, jnp.where(at_panel, row_u[:, None], factor_u))
         factor_v = jnp.where(update_mask, fresh_v, jnp.where(at_panel, row_v[:, None], factor_v))
-        self_c = jnp.einsum(
-            "arx,asx->ars", row_v, row_v, preferred_element_type=jnp.float32
-        ).astype(jnp.bfloat16)
-        spread = jnp.einsum(
-            "ars,asx->arx", self_c, row_u, preferred_element_type=jnp.float32
-        ).astype(jnp.bfloat16)
-        part_u = lax.dynamic_slice_in_dim(row_u, first_row, diag_rows, 2)
-        lowered = diagonal - jnp.einsum(
-            "arx,ary->axy", part_u, spread, preferred_element_type=jnp.float32
-        )
-        chol_rows = lax.dynamic_slice_in_dim(chol_k, first_row, diag_rows, 0)
-        diag_tile = row_tile[:, None, None]
-        diagonal = jnp.where(
-            diag_tile > panel_index,
-            lowered,
-            jnp.where(diag_tile == panel_index, chol_rows[None], diagonal),
-        )
     return (factor_u, factor_v, diagonal)
 
 

time: 1430 us -> 1270 us (0.89)
  other arithmetic: 400 us -> 243 us
  local copies, waits for them, and re-layouts: 78.8 us -> 63.5 us
    another operation x5 -> x0, other arithmetic: 170 us -> none  [solve_panel(): solved = jax.scipy.linalg.solve_triangular(chol_k, flattened, lower=True)]
    another operation x53 -> x2, local copies, waits for them, and re-layouts: 62.8 us -> 5.04 us  [the longest x51 57.7 us: solve_panel(): solved = jax.scipy.linalg.solve_triangular(chol_k, flattened, lower=True)]
    all_gather x2 -> x1, waiting for transfers between devices: 106 us -> 50.7 us  [on_device(): whole_tile = lax.all_gather(diagonal[diag_slot], 'col', axis=0, tiled=True)]
    dot_general x0 -> x30, matrix products: none -> 54.5 us  [the longest x14 30.3 us: solve_packed(): rhs = rhs - jnp.dot(prior, packed[lo:hi, :lo].T, precision=highest)]
    another operation x30 -> x0, matrix products: 38.2 us -> none  [solve_panel(): solved = jax.scipy.linalg.solve_triangular(chol_k, flattened, lower=True)]
    all_gather x0 -> x1, waiting for transfers between devices: none -> 33.4 us  [on_device(): whole_tile = lax.all_gather(diagonal[next_slot], 'col', axis=0, tiled=True)]
    psum x6, waiting for transfers between devices: 721 us -> 744 us  [broadcast(): return lax.psum(jnp.where(mine, shard, jnp.zeros_like(shard)), axis)]
    gather x0 -> x16, local copies, waits for them, and re-layouts: none -> 20.6 us  [solve_packed(): inverse = jnp.tril(block.T, -1) + jnp.diag(1.0 / jnp.diagonal(block))]
  transfers between devices with their start and end apart: 8 -> 8, of which waited for: 8 -> 8; matrix products, arithmetic and copies ran while one was open for 3% -> 4% of each run, Pallas kernels for 0% -> 0%
where the time goes in v2:
time: 1270 us; the launch traced here: 1260 us
  waiting for transfers between devices  828 us (65%)
  other arithmetic  243 us (19%)
  matrix products  100 us (8%)
  local copies, waits for them, and re-layouts  63.5 us (5%)
  between operations  16.2 us (1%)
    psum x6, waiting for transfers between devices, broadcast(): return lax.psum(jnp.where(mine, shard, jnp.zeros_like(shard)), axis)  744 us
    another operation x18, other arithmetic, on_device(): gram_chol = jnp.linalg.cholesky(gram_matrix)  119 us
    another operation x11, other arithmetic, on_device(): jax.scipy.linalg.solve_triangular(gram_chol, jnp.broadcast_to(identity, g...  87 us
    all_gather x1, waiting for transfers between devices, on_device(): whole_tile = lax.all_gather(diagonal[diag_slot], 'col', axis=0, tiled=True)  50.7 us
    all_gather x1, waiting for transfers between devices, on_device(): whole_tile = lax.all_gather(diagonal[next_slot], 'col', axis=0, tiled=True)  33.4 us
    dot_general x14, matrix products, solve_packed(): rhs = rhs - jnp.dot(prior, packed[lo:hi, :lo].T, precision=highest)  30.3 us
  transfers between devices with their start and end apart: 8, of which 8 were waited for; matrix products, arithmetic and copies ran while one was open for 4% of the time, Pallas kernels for 0%

profile of v2, /device:TPU:37, one launch (start us, length us, event | category | flops | bytes accessed | tf_op | source)
XLA Modules:
  0.0 1260.4 jit_solution(2433032225718311677)
XLA Ops:
  13.1 50.7 %all-gather.5.cloned.1.call-done = f32[1,1024,1024]{2,0,1:T(1,128)} async-done(((f32[1,64,1024]{2,0,1:T(1,128)}), f32[1,1024,1024]{2,0,1:T(1,128)}) %all-gather.5.cloned.1.call-update) | async-done | bytes 4194320 | tf_op jit(solution)/shard_map/all_gather | solution.py:109
  63.8 5.2 copy.421
  70.3 6.4 conditional.2
  76.8 79.6 %all-reduce.22.cloned.1.call-done = (bf16[2,192,1024]{2,1,0:T(8,128)(2,1)}, bf16[2,192,1024]{2,1,0:T(8,128)(2,1)}) async-done(((bf16[2,192,1024]{2,1,0:T(8,128)(2,1)}, bf16[2,192,1024]{2,1,0:T(8,128)(2,1)}), (bf16[2,192,1024]{2,1,0:T(8,128)(2,1)}, bf16[2,192,1024]{2,1,0:T(8,128)(2,1)})) %all-reduce.22.cloned.1.call-update) | async-done | bytes 1572880 | tf_op jit(solution)/shard_map/psum | solution.py:14
  160.0 2.9 broadcast_select_fusion.1
  164.1 234.8 %all-reduce.26.cloned.1.call-done = (bf16[1,192,1024]{2,1,0:T(8,128)(2,1)}, bf16[1,192,1024]{2,1,0:T(8,128)(2,1)}) async-done(((bf16[1,192,1024]{2,1,0:T(8,128)(2,1)}, bf16[1,192,1024]{2,1,0:T(8,128)(2,1)}), (bf16[1,192,1024]{2,1,0:T(8,128)(2,1)}, bf16[1,192,1024]{2,1,0:T(8,128)(2,1)})) %all-reduce.26.cloned.1.call-update) | async-done | bytes 786448 | tf_op jit(solution)/shard_map/psum | solution.py:14
  403.1 70.6 %all-reduce.16.cloned.1.call-done = f32[1024,1024]{1,0:T(8,128)} async-done(((f32[1024,1024]{1,0:T(8,128)}), f32[1024,1024]{1,0:T(8,128)}) %all-reduce.16.cloned.1.call-update) | async-done | bytes 4194320 | tf_op jit(solution)/shard_map/psum | solution.py:14
  508.7 2.5 convolution_subtract_fusion.14
  512.5 2.9 convolution_subtract_fusion.13
  542.8 33.4 %all-gather.7.cloned.1.call-done = f32[1,1024,1024]{2,1,0:T(8,128)} async-done(((f32[1,64,1024]{2,1,0:T(8,128)}), f32[1,1024,1024]{2,1,0:T(8,128)}) %all-gather.7.cloned.1.call-update) | async-done | bytes 4194320 | tf_op jit(solution)/shard_map/all_gather | solution.py:163
  576.4 23.5 %custom-call.117 = f32[2,1,128,128]{3,2,1,0:T(8,128)S(1)} custom-call(f32[2,1,128,128]{3,2,1,0:T(8,128)S(1)} %slice_bitcast_fusion.14), custom_call_target="Cholesky" | custom-call | tf_op jit(solution)/shard_map/jit(cholesky)/cholesky | solution.py:191
  600.5 19.7 %custom-call.118 = f32[2,1,1,128,128]{3,4,2,1,0:T(8,128)S(1)} custom-call(f32[2,1,1,128,128]{4,3,2,1,0:T(8,128)S(1)} %get-tuple-element.168), custom_call_target="InvertDiagBlocksLowerTriangular" | custom-call | tf_op jit(solution)/shard_map/jit(cholesky)/cholesky | solution.py:191
  621.6 11.7 custom-call.119
  637.7 40.9 %custom-call.120 = f32[2,2,128,128]{2,3,1,0:T(8,128)} custom-call(f32[2,2,128,128]{3,2,1,0:T(8,128)} %pad_maximum_fusion.8), custom_call_target="InvertDiagBlocksLowerTriangular" | custom-call | tf_op jit(solution)/shard_map/jit(_solve_triangular)/vmap()/triangular_solve | solution.py:192
  689.2 7.2 conditional.3
  696.4 78.8 %all-reduce.20.cloned.1.call-done = (bf16[2,192,1024]{2,1,0:T(8,128)(2,1)}, bf16[2,192,1024]{2,1,0:T(8,128)(2,1)}) async-done(((bf16[2,192,1024]{2,1,0:T(8,128)(2,1)}, bf16[2,192,1024]{2,1,0:T(8,128)(2,1)}), (bf16[2,192,1024]{2,1,0:T(8,128)(2,1)}, bf16[2,192,1024]{2,1,0:T(8,128)(2,1)})) %all-reduce.20.cloned.1.call-update) | async-done | bytes 1572880 | tf_op jit(solution)/shard_map/psum | solution.py:14
  778.8 2.9 broadcast_select_fusion
  787.8 209.5 %all-reduce.24.cloned.1.call-done = (bf16[1,192,1024]{2,1,0:T(8,128)(2,1)}, bf16[1,192,1024]{2,1,0:T(8,128)(2,1)}) async-done(((bf16[1,192,1024]{2,1,0:T(8,128)(2,1)}, bf16[1,192,1024]{2,1,0:T(8,128)(2,1)}), (bf16[1,192,1024]{2,1,0:T(8,128)(2,1)}, bf16[1,192,1024]{2,1,0:T(8,128)(2,1)})) %all-reduce.24.cloned.1.call-update) | async-done | bytes 786448 | tf_op jit(solution)/shard_map/psum | solution.py:14
  1001.3 70.9 %all-reduce.18.cloned.1.call-done = f32[1024,1024]{1,0:T(8,128)} async-done(((f32[1024,1024]{1,0:T(8,128)}), f32[1024,1024]{1,0:T(8,128)}) %all-reduce.18.cloned.1.call-update) | async-done | bytes 4194320 | tf_op jit(solution)/shard_map/psum | solution.py:14
  1110.7 2.9 convolution_subtract_fusion.8
  1124.7 24.9 %custom-call.121 = f32[2,1,128,128]{3,2,1,0:T(8,128)} custom-call(f32[2,1,128,128]{3,2,1,0:T(8,128)} %cholesky.255), custom_call_target="Cholesky" | custom-call | tf_op jit(solution)/shard_map/jit(cholesky)/cholesky | solution.py:191
  1152.9 21.1 %custom-call.122 = f32[2,1,1,128,128]{3,4,2,1,0:T(8,128)} custom-call(f32[2,1,1,128,128]{4,3,2,1,0:T(8,128)} %get-tuple-element.166), custom_call_target="InvertDiagBlocksLowerTriangular" | custom-call | tf_op jit(solution)/shard_map/jit(cholesky)/cholesky | solution.py:191
  1177.5 13.1 %custom-call.123 = f32[2,1,64,64]{3,2,1,0:T(8,128)} custom-call(f32[2,1,64,64]{3,2,1,0:T(8,128)} %fusion.143), custom_call_target="Cholesky" | custom-call | tf_op jit(solution)/shard_map/jit(cholesky)/cholesky | solution.py:191
  1198.3 41.0 %custom-call.124 = f32[2,2,128,128]{2,3,1,0:T(8,128)} custom-call(f32[2,2,128,128]{3,2,1,0:T(8,128)} %pad_maximum_fusion.9), custom_call_target="InvertDiagBlocksLowerTriangular" | custom-call | tf_op jit(solution)/shard_map/jit(_solve_triangular)/vmap()/triangular_solve | solution.py:192
  (355 shorter events, 192.4 us)
Async XLA Ops:
  7.2 525.5 %copy-start = (bf16[192,1024]{1,0:T(8,128)(2,1)S(1)}, bf16[192,1024]{1,0:T(8,128)(2,1)}, u32[]{:S(2)}) copy-start(bf16[192,1024]{1,0:T(8,128)(2,1)} %param.18) | copy-start | bytes 1179652
  7.2 56.6 %all-gather.5.cloned.1.call-start = ((), (), s32[]{:S(2)}) async-start(), calls=%async_computation.2 | async-start | bytes 4456448 | tf_op jit(solution)/shard_map/all_gather | solution.py:109
  9.2 147.2 %all-reduce.22.cloned.1.call-start = ((), (), s32[]{:S(2)}) async-start(), calls=%async_computation.5 | async-start | bytes 3145728 | tf_op jit(solution)/shard_map/psum | solution.py:14
  11.6 57.4 %copy-start.78 = (pred[2,192]{1,0:T(4,128)(4,1)}, pred[2,192]{1,0:T(4,128)(4,1)S(1)}, u32[]{:S(2)}) copy-start(pred[2,192]{1,0:T(4,128)(4,1)S(1)} %compare_and_fusion) | copy-start | bytes 1156
  70.3 328.7 %all-reduce.26.cloned.1.call-start = ((), (), s32[]{:S(2)}) async-start(), calls=%async_computation.7 | async-start | bytes 1572864 | tf_op jit(solution)/shard_map/psum | solution.py:14
  160.0 313.7 %all-reduce.16.cloned.1.call-start = ((), (), s32[]{:S(2)}) async-start(), calls=%async_computation | async-start | bytes 8388608 | tf_op jit(solution)/shard_map/psum | solution.py:14
  162.9 413.2 %all-gather.7.cloned.1.call-start = ((), (), s32[]{:S(2)}) async-start(), calls=%async_computation.3 | async-start | bytes 4456448 | tf_op jit(solution)/shard_map/all_gather | solution.py:163
  163.0 355.1 %copy-start.90 = (s32[64]{0:T(128)}, s32[64]{0:T(128)S(1)}, u32[]{:S(2)}) copy-start(s32[64]{0:T(128)S(1)} %iota_add_fusion) | copy-start | bytes 772
  163.5 355.6 %copy-start.82 = (pred[2]{0:T(512)(128)(4,1)}, pred[2]{0:T(512)(128)(4,1)S(1)}, u32[]{:S(2)}) copy-start(pred[2]{0:T(512)(128)(4,1)S(1)} %get-tuple-element.206) | copy-start | bytes 10
  520.8 14.2 %copy-start.20 = (f32[2,64,1024]{2,1,0:T(8,128)}, f32[2,64,1024]{2,1,0:T(8,128)S(1)}, u32[]{:S(2)}) copy-start(f32[2,64,1024]{2,1,0:T(8,128)S(1)} %fusion.107) | copy-start | bytes 1572868
  521.5 253.7 %all-reduce.20.cloned.1.call-start = ((), (), s32[]{:S(2)}) async-start(), calls=%async_computation.4 | async-start | bytes 3145728 | tf_op jit(solution)/shard_map/psum | solution.py:14
  521.8 13.2 %copy-start.26 = (f32[192,192]{0,1:T(8,128)}, f32[192,192]{0,1:T(8,128)S(1)}, u32[]{:S(2)}) copy-start(f32[192,192]{0,1:T(8,128)S(1)} %fusion.211) | copy-start | bytes 442372
  542.4 57.5 %copy-start.76 = (pred[128,128]{1,0:T(8,128)(4,1)S(1)}, pred[128,128]{1,0:T(8,128)(4,1)}, u32[]{:S(2)}) copy-start(pred[128,128]{1,0:T(8,128)(4,1)} %get-tuple-element.209) | copy-start | bytes 49156
  542.4 57.5 %copy-start.77 = (pred[128,128]{1,0:T(8,128)(4,1)S(1)}, pred[128,128]{1,0:T(8,128)(4,1)}, u32[]{:S(2)}) copy-start(pred[128,128]{1,0:T(8,128)(4,1)} %get-tuple-element.210) | copy-start | bytes 49156
  576.4 43.8 %copy-start.51 = (f32[2,1,192,192]{3,2,0,1:T(8,128)}, f32[2,1,192,192]{3,2,0,1:T(8,128)S(1)}, u32[]{:S(2)}) copy-start(f32[2,1,192,192]{3,2,0,1:T(8,128)S(1)} %fusion.191) | copy-start | bytes 884740
  576.4 102.3 %copy-start.45 = (f32[128,192]{1,0:T(8,128)S(1)}, f32[128,192]{1,0:T(8,128)}, u32[]{:S(2)}) copy-start(f32[128,192]{1,0:T(8,128)} %copy.418) | copy-start | bytes 294916
  600.5 79.8 %copy-start.61 = (f32[64,192]{1,0:T(8,128)S(1)}, f32[64,192]{1,0:T(8,128)}, u32[]{:S(2)}) copy-start(f32[64,192]{1,0:T(8,128)} %copy.419) | copy-start | bytes 147460
  620.4 62.5 %copy-start.41 = (f32[2,1,192,192]{3,2,0,1:T(8,128)S(1)}, f32[2,1,192,192]{3,2,0,1:T(8,128)}, u32[]{:S(2)}) copy-start(f32[2,1,192,192]{3,2,0,1:T(8,128)} %convolution_bitcast_fusion.5) | copy-start | bytes 884740
  620.4 62.5 %copy-start.43 = (f32[2,1,192,192]{3,2,0,1:T(8,128)S(1)}, f32[2,1,192,192]{3,2,0,1:T(8,128)}, u32[]{:S(2)}) copy-start(f32[2,1,192,192]{3,2,0,1:T(8,128)} %convolution_bitcast_fusion.6) | copy-start | bytes 884740
  636.9 44.7 %copy-start.46 = (f32[2,128,64]{2,1,0:T(8,128)}, f32[2,128,64]{2,1,0:T(8,128)S(1)}, u32[]{:S(2)}) copy-start(f32[2,128,64]{2,1,0:T(8,128)S(1)} %triangular_solve.138) | copy-start | bytes 196612
  678.7 6.2 copy-start.62
  689.2 308.0 %all-reduce.24.cloned.1.call-start = ((), (), s32[]{:S(2)}) async-start(), calls=%async_computation.6 | async-start | bytes 1572864 | tf_op jit(solution)/shard_map/psum | solution.py:14
  778.8 293.3 %all-reduce.18.cloned.1.call-start = ((), (), s32[]{:S(2)}) async-start(), calls=%async_computation.1 | async-start | bytes 8388608 | tf_op jit(solution)/shard_map/psum | solution.py:14
  786.9 210.3 %copy-start.40 = (bf16[2,192,1024]{2,1,0:T(8,128)(2,1)S(1)}, bf16[2,192,1024]{2,1,0:T(8,128)(2,1)}, u32[]{:S(2)}) copy-start(bf16[2,192,1024]{2,1,0:T(8,128)(2,1)} %get-tuple-element.74) | copy-start | bytes 2359300
  (56 other events, 132.7 us)
Sparse Core Ops, SparseCore 0:
  10.7 53.0 all-gather.4
  70.4 85.9 all-reduce.21
  160.1 238.8 all-reduce.25
  401.2 72.4 all-reduce.15
  521.7 54.4 all-gather.6
  689.3 85.8 all-reduce.19
  778.9 218.2 all-reduce.23
  999.6 72.4 all-reduce.17

commit v3 on v2

--- a/solution.py
+++ b/solution.py
@@ -46,6 +46,27 @@
             parts.append(below)
         strips.append(jnp.concatenate(parts, axis=0))
     return jnp.concatenate(strips, axis=1)
+
+
+def factor_inverse(gram):
+    order = gram.shape[-1]
+    width = min(BLOCK, order)
+    gram = (gram + jnp.swapaxes(gram, -1, -2)) * 0.5
+    eye = jnp.broadcast_to(jnp.eye(width, dtype=jnp.float32), gram.shape[:-2] + (width, width))
+    head = jnp.tril(lax.linalg.cholesky(gram[..., :width, :width], symmetrize_input=False))
+    head_inv = lax.linalg.triangular_solve(head, eye, left_side=True, lower=True)
+    if width == order:
+        return head_inv
+    rest = order - width
+    below = jnp.einsum("...ij,...kj->...ik", gram[..., width:, :width], head_inv, precision=highest)
+    tail = gram[..., width:, width:] - jnp.einsum("...ij,...kj->...ik", below, below, precision=highest)
+    tail = jnp.tril(lax.linalg.cholesky(tail, symmetrize_input=False))
+    eye_rest = jnp.broadcast_to(jnp.eye(rest, dtype=jnp.float32), gram.shape[:-2] + (rest, rest))
+    tail_inv = lax.linalg.triangular_solve(tail, eye_rest, left_side=True, lower=True)
+    cross = jnp.einsum("...ij,...jk->...ik", below, head_inv, precision=highest)
+    cross = -jnp.einsum("...ij,...jk->...ik", tail_inv, cross, precision=highest)
+    top = jnp.concatenate([head_inv, jnp.zeros(gram.shape[:-2] + (width, rest), jnp.float32)], -1)
+    return jnp.concatenate([top, jnp.concatenate([cross, tail_inv], -1)], -2)
 
 
 def solve_packed(packed, raw_factors):
@@ -124,13 +145,19 @@
             1,
             keepdims=False,
         )
-        col_u, col_raw = (
-            broadcast(relay_u, "row", col_index % row_count),
-            broadcast(relay_v, "row", col_index % row_count),
-        )
         own_chol = lax.cond(row_index == diag_owner, factor_tile, zero_tile, whole_tile)
         whole_tile = None
-        chol_k = broadcast(own_chol, "row", diag_owner)
+        relay_here = row_index == col_index % row_count
+        relay = jnp.concatenate([relay_u, relay_v], axis=0).astype(jnp.float32)
+        relay = jnp.where(relay_here, relay, jnp.zeros_like(relay))
+        own_chol = jnp.where(row_index == diag_owner, own_chol, jnp.zeros_like(own_chol))
+        merged = lax.psum(
+            jnp.concatenate([own_chol, relay.reshape(-1, tile_order)], axis=0), "row"
+        )
+        chol_k = merged[:tile_order]
+        relay = merged[tile_order:].reshape(relay.shape).astype(jnp.bfloat16)
+        col_u = relay[:tiles_col]
+        col_raw = relay[tiles_col:]
         solved = solve_packed(chol_k, jnp.concatenate([row_raw, col_raw], axis=0))
         row_v = solved[:tiles_row]
         col_v = solved[tiles_row:]
@@ -181,17 +208,12 @@
             "abrx,absx->abrs", range_y, range_y, preferred_element_type=jnp.float32
         )
         gram_matrix = gram_matrix + (1.0 - keep_rows.astype(jnp.float32))[..., None] * identity
-        if whole_tile is not None:
-            whole_tile, gram_matrix = lax.optimization_barrier((whole_tile, gram_matrix))
         proj_u = jnp.einsum(
             "abrx,absx->abrs", range_y, factor_u, preferred_element_type=jnp.float32
         )
         proj_own = jnp.einsum("abrx,asx->abrs", range_y, row_u, preferred_element_type=jnp.float32)
         proj_c = jnp.einsum("abrs,abst->abrt", proj_own, coupling, precision=highest)
-        gram_chol = jnp.linalg.cholesky(gram_matrix)
-        gram_inv = jax.scipy.linalg.solve_triangular(
-            gram_chol, jnp.broadcast_to(identity, gram_chol.shape), lower=True
-        )
+        gram_inv = factor_inverse(gram_matrix)
         both = jnp.concatenate([proj_u, proj_c], axis=-1)
         middle = jnp.einsum("abrs,abst->abrt", gram_inv, both, precision=highest)
         cores = jnp.einsum("absr,abst->abrt", gram_inv, middle, precision=highest)

time: 1270 us -> 1120 us (0.88)
  waiting for transfers between devices: 828 us -> 704 us
  other arithmetic: 243 us -> 205 us
  local copies, waits for them, and re-layouts: 63.5 us -> 82 us
    psum x6 -> x2, waiting for transfers between devices: 744 us -> 149 us  [broadcast(): return lax.psum(jnp.where(mine, shard, jnp.zeros_like(shard)), axis)]
    psum x0 -> x2, waiting for transfers between devices: none -> 505 us  [on_device(): lax.psum(jnp.concatenate([own_chol, relay.reshape(-1, tile_order)], axis=...]
    another operation x29 -> x26, other arithmetic: 206 us -> 152 us  [the longest x7 51.1 us: factor_inverse(): lax.linalg.cholesky(gram[..., :width, :width], symmetrize_input=False)]
    all_gather x1, waiting for transfers between devices: 33.4 us -> 0.01 us  [on_device(): whole_tile = lax.all_gather(diagonal[next_slot], 'col', axis=0, tiled=True)]
    gather x16, local copies, waits for them, and re-layouts: 20.6 us -> 34.9 us  [solve_packed(): inverse = jnp.tril(block.T, -1) + jnp.diag(1.0 / jnp.diagonal(block))]
  transfers between devices with their start and end apart: 8 -> 6, of which waited for: 8 -> 5; matrix products, arithmetic and copies ran while one was open for 4% -> 11% of each run, Pallas kernels for 0% -> 0%
where the time goes in v3:
time: 1120 us; the launch traced here: 1110 us
  waiting for transfers between devices  704 us (63%)
  other arithmetic  205 us (18%)
  matrix products  90.7 us (8%)
  local copies, waits for them, and re-layouts  82 us (7%)
  between operations  15.7 us (1%)
  loops' own time  13.4 us (1%)
    psum x2, waiting for transfers between devices, on_device(): lax.psum(jnp.concatenate([own_chol, relay.reshape(-1, tile_order)], axis=...  505 us
    psum x2, waiting for transfers between devices, broadcast(): return lax.psum(jnp.where(mine, shard, jnp.zeros_like(shard)), axis)  149 us
    another operation x7, other arithmetic, factor_inverse(): lax.linalg.cholesky(gram[..., :width, :width], symmetrize_input=False)  51.1 us
    all_gather x1, waiting for transfers between devices, on_device(): whole_tile = lax.all_gather(diagonal[diag_slot], 'col', axis=0, tiled=True)  50.7 us
    another operation x5, other arithmetic, factor_inverse(): lax.linalg.triangular_solve(head, eye, left_side=True, lower=True)  44.1 us
    gather x16, local copies, waits for them, and re-layouts, solve_packed(): inverse = jnp.tril(block.T, -1) + jnp.diag(1.0 / jnp.diagonal(block))  34.9 us
    another operation x7, other arithmetic, factor_inverse(): tail = jnp.tril(lax.linalg.cholesky(tail, symmetrize_input=False))  27.3 us
    dot_general x14, matrix products, solve_packed(): rhs = rhs - jnp.dot(prior, packed[lo:hi, :lo].T, precision=highest)  26.4 us
  transfers between devices with their start and end apart: 6, of which 5 were waited for; matrix products, arithmetic and copies ran while one was open for 11% of the time, Pallas kernels for 0%

profile of v3, /device:TPU:37, one launch (start us, length us, event | category | flops | bytes accessed | tf_op | source)
XLA Modules:
  0.0 1111.4 jit_solution(18048250334852695739)
XLA Ops:
  13.1 50.7 %all-gather.5.cloned.1.call-done = f32[1,1024,1024]{2,0,1:T(1,128)} async-done(((f32[1,64,1024]{2,0,1:T(1,128)}), f32[1,1024,1024]{2,0,1:T(1,128)}) %all-gather.5.cloned.1.call-update) | async-done | bytes 4194320 | tf_op jit(solution)/shard_map/all_gather | solution.py:130
  63.8 5.2 copy.417
  70.3 12.7 %conditional.2 = (f32[1024,1024]{1,0:T(8,128)}) conditional(s32[]{:T(128)} %convert_element_type.173, () %tuple.29, f32[1024,1024]{1,0:T(8,128)} %bitcast.703), branch_computations={%region_2.3_spmd, %region_3.8_spmd} | conditional | flops 4437377024 | bytes 110301656 | solution.py:148
  83.0 2.8 broadcast_select_fusion.1
  85.8 70.5 %all-reduce.17.cloned.1.call-done = (bf16[2,192,1024]{2,1,0:T(8,128)(2,1)}, bf16[2,192,1024]{2,1,0:T(8,128)(2,1)}) async-done(((bf16[2,192,1024]{2,1,0:T(8,128)(2,1)}, bf16[2,192,1024]{2,1,0:T(8,128)(2,1)}), (bf16[2,192,1024]{2,1,0:T(8,128)(2,1)}, bf16[2,192,1024]{2,1,0:T(8,128)(2,1)})) %all-reduce.17.cloned.1.call-update) | async-done | bytes 1572880 | tf_op jit(solution)/shard_map/psum | solution.py:14
  158.6 5.8 pad_maximum_fusion
  166.3 243.7 %all-reduce.11.cloned.1.call-done = f32[1408,1024]{1,0:T(8,128)} async-done(((f32[1408,1024]{1,0:T(8,128)}), f32[1408,1024]{1,0:T(8,128)}) %all-reduce.11.cloned.1.call-update) | async-done | bytes 5767184 | tf_op jit(solution)/shard_map/psum | solution.py:154
  410.0 3.2 convert.62
  457.7 2.8 convolution_subtract_fusion.15
  492.6 25.0 %custom-call.116 = f32[2,1,128,128]{3,2,1,0:T(8,128)} custom-call(f32[2,1,128,128]{3,2,1,0:T(8,128)} %slice.587), custom_call_target="Cholesky" | custom-call | tf_op jit(solution)/shard_map/cholesky/custom-call.0 | solution.py:56
  520.4 21.1 %custom-call.117 = f32[2,1,1,128,128]{3,4,2,1,0:T(8,128)} custom-call(f32[2,1,1,128,128]{4,3,2,1,0:T(8,128)} %fusion.241), custom_call_target="InvertDiagBlocksLowerTriangular" | custom-call | tf_op jit(solution)/shard_map/triangular_solve/custom-call.4 | solution.py:57
  546.8 13.1 %custom-call.118 = f32[2,1,64,64]{3,2,1,0:T(8,128)} custom-call(f32[2,1,64,64]{3,2,1,0:T(8,128)} %fusion.143), custom_call_target="Cholesky" | custom-call | tf_op jit(solution)/shard_map/cholesky/custom-call.2 | solution.py:63
  562.4 11.4 %custom-call.119 = f32[2,1,1,64,64]{3,4,2,1,0:T(8,128)} custom-call(f32[2,1,1,64,64]{4,3,2,1,0:T(8,128)} %fusion.281), custom_call_target="InvertDiagBlocksLowerTriangular" | custom-call | tf_op jit(solution)/shard_map/triangular_solve/custom-call.5 | solution.py:65
  582.5 3.8 bitcast_select_fusion.18
  586.4 5.8 conditional.3
  592.2 2.8 broadcast_select_fusion
  595.0 78.1 %all-reduce.15.cloned.1.call-done = (bf16[2,192,1024]{2,1,0:T(8,128)(2,1)}, bf16[2,192,1024]{2,1,0:T(8,128)(2,1)}) async-done(((bf16[2,192,1024]{2,1,0:T(8,128)(2,1)}, bf16[2,192,1024]{2,1,0:T(8,128)(2,1)}), (bf16[2,192,1024]{2,1,0:T(8,128)(2,1)}, bf16[2,192,1024]{2,1,0:T(8,128)(2,1)})) %all-reduce.15.cloned.1.call-update) | async-done | bytes 1572880 | tf_op jit(solution)/shard_map/psum | solution.py:14
  675.3 5.8 pad_maximum_fusion.1
  685.3 261.3 %all-reduce.13.cloned.1.call-done = f32[1408,1024]{1,0:T(8,128)} async-done(((f32[1408,1024]{1,0:T(8,128)}), f32[1408,1024]{1,0:T(8,128)}) %all-reduce.13.cloned.1.call-update) | async-done | bytes 5767184 | tf_op jit(solution)/shard_map/psum | solution.py:154
  946.6 3.2 convert.72
  1016.4 23.5 %custom-call.120 = f32[2,1,128,128]{3,2,1,0:T(8,128)S(1)} custom-call(f32[2,1,128,128]{3,2,1,0:T(8,128)S(1)} %slice.619), custom_call_target="Cholesky" | custom-call | tf_op jit(solution)/shard_map/cholesky/custom-call.0 | solution.py:56
  1041.6 19.9 %custom-call.121 = f32[2,1,1,128,128]{3,4,2,1,0:T(8,128)S(1)} custom-call(f32[2,1,1,128,128]{4,3,2,1,0:T(8,128)S(1)} %fusion.235), custom_call_target="InvertDiagBlocksLowerTriangular" | custom-call | tf_op jit(solution)/shard_map/triangular_solve/custom-call.4 | solution.py:57
  1070.0 12.5 %custom-call.122 = f32[2,1,64,64]{3,2,1,0:T(8,128)S(1)} custom-call(f32[2,1,64,64]{3,2,1,0:T(8,128)} %fusion.144), custom_call_target="Cholesky" | custom-call | tf_op jit(solution)/shard_map/cholesky/custom-call.2 | solution.py:63
  1082.7 9.8 custom-call.123
  (365 shorter events, 206.4 us)
Async XLA Ops:
  7.2 472.2 %copy-start = (bf16[192,1024]{1,0:T(8,128)(2,1)S(1)}, bf16[192,1024]{1,0:T(8,128)(2,1)}, u32[]{:S(2)}) copy-start(bf16[192,1024]{1,0:T(8,128)(2,1)} %param.21) | copy-start | bytes 1179652
  7.2 56.6 %all-gather.5.cloned.1.call-start = ((), (), s32[]{:S(2)}) async-start(), calls=%async_computation.2 | async-start | bytes 4456448 | tf_op jit(solution)/shard_map/all_gather | solution.py:130
  9.2 147.1 %all-reduce.17.cloned.1.call-start = ((), (), s32[]{:S(2)}) async-start(), calls=%async_computation.5 | async-start | bytes 3145728 | tf_op jit(solution)/shard_map/psum | solution.py:14
  11.6 57.4 %copy-start.81 = (pred[2,192]{1,0:T(4,128)(4,1)}, pred[2,192]{1,0:T(4,128)(4,1)S(1)}, u32[]{:S(2)}) copy-start(pred[2,192]{1,0:T(4,128)(4,1)S(1)} %compare_and_fusion) | copy-start | bytes 1156
  13.1 55.8 %copy-start.5 = (bf16[2,192,1024]{2,1,0:T(8,128)(2,1)}, bf16[2,192,1024]{2,1,0:T(8,128)(2,1)S(1)}, u32[]{:S(2)}) copy-start(bf16[2,192,1024]{2,1,0:T(8,128)(2,1)S(1)} %get-tuple-element.22) | copy-start | bytes 2359300
  70.2 339.7 %all-reduce.11.cloned.1.call-start = ((), (), s32[]{:S(2)}) async-start(), calls=%async_computation | async-start | bytes 11534336 | tf_op jit(solution)/shard_map/psum | solution.py:154
  164.4 418.1 %all-gather.7.cloned.1.call-start = ((), (), s32[]{:S(2)}) async-start(), calls=%async_computation.3 | async-start | bytes 4456448 | tf_op jit(solution)/shard_map/all_gather | solution.py:190
  166.2 304.3 %copy-start.82 = (pred[2]{0:T(512)(128)(4,1)}, pred[2]{0:T(512)(128)(4,1)S(1)}, u32[]{:S(2)}) copy-start(pred[2]{0:T(512)(128)(4,1)S(1)} %get-tuple-element.172) | copy-start | bytes 10
  421.9 33.4 %slice-start.3 = ((s8[5767168]{0:T(1024)(128)(4,1)}), s8[1572864]{0:T(1024)(128)(4,1)S(1)}, s32[]{:S(2)}) async-start(s8[5767168]{0:T(1024)(128)(4,1)} %bitcast.706), calls=%async_computation.9 | async-start | bytes 3145728
  440.9 6.6 copy-start.106
  444.3 10.9 slice-start.4
  470.3 9.0 copy-start.6
  472.2 9.5 copy-start.33
  473.0 200.1 %all-reduce.15.cloned.1.call-start = ((), (), s32[]{:S(2)}) async-start(), calls=%async_computation.4 | async-start | bytes 3145728 | tf_op jit(solution)/shard_map/psum | solution.py:14
  586.3 96.6 %copy-start.38 = (bf16[2,1,192,1024]{3,2,0,1:T(8,128)(2,1)}, bf16[2,1,192,1024]{3,2,0,1:T(8,128)(2,1)S(1)}, u32[]{:S(2)}) copy-start(bf16[2,1,192,1024]{3,2,0,1:T(8,128)(2,1)S(1)} %get-tuple-element.52) | copy-start | bytes 2359300
  586.3 360.3 %all-reduce.13.cloned.1.call-start = ((), (), s32[]{:S(2)}) async-start(), calls=%async_computation.1 | async-start | bytes 11534336 | tf_op jit(solution)/shard_map/psum | solution.py:154
  958.8 40.0 %slice-start = ((s8[5767168]{0:T(1024)(128)(4,1)}), s8[1572864]{0:T(1024)(128)(4,1)S(1)}, s32[]{:S(2)}) async-start(s8[5767168]{0:T(1024)(128)(4,1)} %bitcast.704), calls=%async_computation.6 | async-start | bytes 3145728
  984.4 6.6 copy-start.105
  987.9 11.0 slice-start.1
  1062.6 32.2 %copy-start.35 = (f32[2,128,128]{1,2,0:T(8,128)}, f32[2,128,128]{1,2,0:T(8,128)S(1)}, u32[]{:S(2)}) copy-start(f32[2,128,128]{1,2,0:T(8,128)S(1)} %fusion.230) | copy-start | bytes 393220
  1067.0 15.5 %copy-start.80 = (pred[64,64]{1,0:T(8,128)(4,1)S(1)}, pred[64,64]{1,0:T(8,128)(4,1)}, u32[]{:S(2)}) copy-start(pred[64,64]{1,0:T(8,128)(4,1)} %iota_compare_fusion.60) | copy-start | bytes 12292
  1067.0 25.6 %copy-start.68 = (f32[64,64]{1,0:T(8,128)S(1)}, f32[64,64]{1,0:T(8,128)}, u32[]{:S(2)}) copy-start(f32[64,64]{1,0:T(8,128)} %fusion.377) | copy-start | bytes 49156
  1067.0 25.9 %copy-start.53 = (f32[2,192,192]{1,2,0:T(8,128)S(1)}, f32[2,192,192]{1,2,0:T(8,128)}, u32[]{:S(2)}) copy-start(f32[2,192,192]{1,2,0:T(8,128)} %copy-done.52) | copy-start | bytes 884740
  1069.2 25.2 %copy-start.74 = (f32[2,64,128]{2,1,0:T(8,128)S(1)}, f32[2,64,128]{2,1,0:T(8,128)}, u32[]{:S(2)}) copy-start(f32[2,64,128]{2,1,0:T(8,128)} %fusion.438) | copy-start | bytes 196612
  (64 other events, 172.3 us)
Sparse Core Ops, SparseCore 0:
  10.7 53.0 all-gather.4
  70.4 85.9 all-reduce.16
  164.5 245.3 all-reduce.10
  473.1 51.5 all-gather.6
  586.4 86.5 all-reduce.14
  681.3 265.2 all-reduce.12

commit v4 on v3

--- a/solution.py
+++ b/solution.py
@@ -7,6 +7,7 @@
 
 
 highest = lax.Precision.HIGHEST
+fine = lax.Precision.HIGH
 
 
 def broadcast(shard, axis, root):
@@ -41,8 +42,8 @@
         head_inv = lax.linalg.triangular_solve(head, eye, left_side=True, lower=True)
         parts = [jnp.zeros((step * width, width), jnp.float32), head + jnp.triu(head_inv.T, 1)]
         if step < count - 1:
-            below = jnp.dot(work[width:, :width], head_inv.T, precision=highest)
-            work = work[width:, width:] - jnp.dot(below, below.T, precision=highest)
+            below = jnp.dot(work[width:, :width], head_inv.T, precision=fine)
+            work = work[width:, width:] - jnp.dot(below, below.T, precision=fine)
             parts.append(below)
         strips.append(jnp.concatenate(parts, axis=0))
     return jnp.concatenate(strips, axis=1)
@@ -83,8 +84,8 @@
         rhs = rows[:, lo:hi]
         if step:
             prior = jnp.concatenate(done, axis=1)
-            rhs = rhs - jnp.dot(prior, packed[lo:hi, :lo].T, precision=highest)
-        done.append(jnp.dot(rhs, inverse.T, precision=highest))
+            rhs = rhs - jnp.dot(prior, packed[lo:hi, :lo].T, precision=fine)
+        done.append(jnp.dot(rhs, inverse.T, precision=fine))
     return jnp.concatenate(done, axis=1).reshape(lead + (order,)).astype(jnp.bfloat16)
 
 

time: 1120 us -> 1100 us (0.982)
  transfers between devices with their start and end apart: 6 -> 6, of which waited for: 5 -> 5; matrix products, arithmetic and copies ran while one was open for 11% -> 12% of each run, Pallas kernels for 0% -> 0%
where the time goes in v4:
time: 1100 us; the launch traced here: 1090 us
  waiting for transfers between devices  696 us (63%)
  other arithmetic  205 us (19%)
  local copies, waits for them, and re-layouts  83.2 us (8%)
  matrix products  81.8 us (7%)
  between operations  15.8 us (1%)
  loops' own time  12.9 us (1%)
    psum x2, waiting for transfers between devices, on_device(): lax.psum(jnp.concatenate([own_chol, relay.reshape(-1, tile_order)], axis=...  496 us
    psum x2, waiting for transfers between devices, broadcast(): return lax.psum(jnp.where(mine, shard, jnp.zeros_like(shard)), axis)  149 us
    another operation x7, other arithmetic, factor_inverse(): lax.linalg.cholesky(gram[..., :width, :width], symmetrize_input=False)  50.9 us
    all_gather x1, waiting for transfers between devices, on_device(): whole_tile = lax.all_gather(diagonal[diag_slot], 'col', axis=0, tiled=True)  50.7 us
    another operation x5, other arithmetic, factor_inverse(): lax.linalg.triangular_solve(head, eye, left_side=True, lower=True)  43.9 us
    gather x16, local copies, waits for them, and re-layouts, solve_packed(): inverse = jnp.tril(block.T, -1) + jnp.diag(1.0 / jnp.diagonal(block))  34.9 us
    another operation x7, other arithmetic, factor_inverse(): tail = jnp.tril(lax.linalg.cholesky(tail, symmetrize_input=False))  27.3 us
    unnamed x174, local copies, waits for them, and re-layouts  25.8 us
  transfers between devices with their start and end apart: 6, of which 5 were waited for; matrix products, arithmetic and copies ran while one was open for 12% of the time, Pallas kernels for 0%

profile of v4, /device:TPU:37, one launch (start us, length us, event | category | flops | bytes accessed | tf_op | source)
XLA Modules:
  0.0 1094.6 jit_solution(3015978092316133230)
XLA Ops:
  13.1 50.7 %all-gather.5.cloned.1.call-done = f32[1,1024,1024]{2,0,1:T(1,128)} async-done(((f32[1,64,1024]{2,0,1:T(1,128)}), f32[1,1024,1024]{2,0,1:T(1,128)}) %all-gather.5.cloned.1.call-update) | async-done | bytes 4194320 | tf_op jit(solution)/shard_map/all_gather | solution.py:131
  63.8 5.2 copy.417
  70.3 12.2 %conditional.2 = (f32[1024,1024]{1,0:T(8,128)}) conditional(s32[]{:T(128)} %convert_element_type.173, () %tuple.29, f32[1024,1024]{1,0:T(8,128)} %bitcast.703), branch_computations={%region_2.3_spmd, %region_3.8_spmd} | conditional | flops 2323448576 | bytes 110301656 | solution.py:149
  82.5 2.8 broadcast_select_fusion.1
  85.3 71.0 %all-reduce.17.cloned.1.call-done = (bf16[2,192,1024]{2,1,0:T(8,128)(2,1)}, bf16[2,192,1024]{2,1,0:T(8,128)(2,1)}) async-done(((bf16[2,192,1024]{2,1,0:T(8,128)(2,1)}, bf16[2,192,1024]{2,1,0:T(8,128)(2,1)}), (bf16[2,192,1024]{2,1,0:T(8,128)(2,1)}, bf16[2,192,1024]{2,1,0:T(8,128)(2,1)})) %all-reduce.17.cloned.1.call-update) | async-done | bytes 1572880 | tf_op jit(solution)/shard_map/psum | solution.py:15
  158.6 5.8 pad_maximum_fusion
  166.3 239.2 %all-reduce.11.cloned.1.call-done = f32[1408,1024]{1,0:T(8,128)} async-done(((f32[1408,1024]{1,0:T(8,128)}), f32[1408,1024]{1,0:T(8,128)}) %all-reduce.11.cloned.1.call-update) | async-done | bytes 5767184 | tf_op jit(solution)/shard_map/psum | solution.py:155
  405.5 3.2 convert.62
  484.2 24.9 %custom-call.116 = f32[2,1,128,128]{3,2,1,0:T(8,128)} custom-call(f32[2,1,128,128]{3,2,1,0:T(8,128)} %slice.587), custom_call_target="Cholesky" | custom-call | tf_op jit(solution)/shard_map/cholesky/custom-call.0 | solution.py:57
  511.8 21.1 %custom-call.117 = f32[2,1,1,128,128]{3,4,2,1,0:T(8,128)} custom-call(f32[2,1,1,128,128]{4,3,2,1,0:T(8,128)} %fusion.241), custom_call_target="InvertDiagBlocksLowerTriangular" | custom-call | tf_op jit(solution)/shard_map/triangular_solve/custom-call.4 | solution.py:58
  538.2 13.1 %custom-call.118 = f32[2,1,64,64]{3,2,1,0:T(8,128)} custom-call(f32[2,1,64,64]{3,2,1,0:T(8,128)} %fusion.143), custom_call_target="Cholesky" | custom-call | tf_op jit(solution)/shard_map/cholesky/custom-call.2 | solution.py:64
  553.8 11.4 %custom-call.119 = f32[2,1,1,64,64]{3,4,2,1,0:T(8,128)} custom-call(f32[2,1,1,64,64]{4,3,2,1,0:T(8,128)} %fusion.281), custom_call_target="InvertDiagBlocksLowerTriangular" | custom-call | tf_op jit(solution)/shard_map/triangular_solve/custom-call.5 | solution.py:66
  573.9 3.8 bitcast_select_fusion.18
  577.8 5.8 conditional.3
  583.6 2.8 broadcast_select_fusion
  586.4 78.0 %all-reduce.15.cloned.1.call-done = (bf16[2,192,1024]{2,1,0:T(8,128)(2,1)}, bf16[2,192,1024]{2,1,0:T(8,128)(2,1)}) async-done(((bf16[2,192,1024]{2,1,0:T(8,128)(2,1)}, bf16[2,192,1024]{2,1,0:T(8,128)(2,1)}), (bf16[2,192,1024]{2,1,0:T(8,128)(2,1)}, bf16[2,192,1024]{2,1,0:T(8,128)(2,1)})) %all-reduce.15.cloned.1.call-update) | async-done | bytes 1572880 | tf_op jit(solution)/shard_map/psum | solution.py:15
  666.7 5.8 pad_maximum_fusion.1
  676.7 256.8 %all-reduce.13.cloned.1.call-done = f32[1408,1024]{1,0:T(8,128)} async-done(((f32[1408,1024]{1,0:T(8,128)}), f32[1408,1024]{1,0:T(8,128)}) %all-reduce.13.cloned.1.call-update) | async-done | bytes 5767184 | tf_op jit(solution)/shard_map/psum | solution.py:155
  933.5 3.2 convert.72
  945.7 2.6 gather_fusion.9
  999.6 23.5 %custom-call.120 = f32[2,1,128,128]{3,2,1,0:T(8,128)S(1)} custom-call(f32[2,1,128,128]{3,2,1,0:T(8,128)S(1)} %slice.619), custom_call_target="Cholesky" | custom-call | tf_op jit(solution)/shard_map/cholesky/custom-call.0 | solution.py:57
  1024.8 19.7 %custom-call.121 = f32[2,1,1,128,128]{3,4,2,1,0:T(8,128)S(1)} custom-call(f32[2,1,1,128,128]{4,3,2,1,0:T(8,128)S(1)} %fusion.235), custom_call_target="InvertDiagBlocksLowerTriangular" | custom-call | tf_op jit(solution)/shard_map/triangular_solve/custom-call.4 | solution.py:58
  1053.0 12.5 %custom-call.122 = f32[2,1,64,64]{3,2,1,0:T(8,128)S(1)} custom-call(f32[2,1,64,64]{3,2,1,0:T(8,128)} %fusion.144), custom_call_target="Cholesky" | custom-call | tf_op jit(solution)/shard_map/cholesky/custom-call.2 | solution.py:64
  1065.7 10.1 custom-call.123
  (365 shorter events, 198.8 us)
Async XLA Ops:
  7.2 463.7 %copy-start = (bf16[192,1024]{1,0:T(8,128)(2,1)S(1)}, bf16[192,1024]{1,0:T(8,128)(2,1)}, u32[]{:S(2)}) copy-start(bf16[192,1024]{1,0:T(8,128)(2,1)} %param.21) | copy-start | bytes 1179652
  7.2 56.6 %all-gather.5.cloned.1.call-start = ((), (), s32[]{:S(2)}) async-start(), calls=%async_computation.2 | async-start | bytes 4456448 | tf_op jit(solution)/shard_map/all_gather | solution.py:131
  9.2 147.1 %all-reduce.17.cloned.1.call-start = ((), (), s32[]{:S(2)}) async-start(), calls=%async_computation.5 | async-start | bytes 3145728 | tf_op jit(solution)/shard_map/psum | solution.py:15
  11.6 57.4 %copy-start.81 = (pred[2,192]{1,0:T(4,128)(4,1)}, pred[2,192]{1,0:T(4,128)(4,1)S(1)}, u32[]{:S(2)}) copy-start(pred[2,192]{1,0:T(4,128)(4,1)S(1)} %compare_and_fusion) | copy-start | bytes 1156
  13.1 55.8 %copy-start.5 = (bf16[2,192,1024]{2,1,0:T(8,128)(2,1)}, bf16[2,192,1024]{2,1,0:T(8,128)(2,1)S(1)}, u32[]{:S(2)}) copy-start(bf16[2,192,1024]{2,1,0:T(8,128)(2,1)S(1)} %get-tuple-element.22) | copy-start | bytes 2359300
  70.2 335.2 %all-reduce.11.cloned.1.call-start = ((), (), s32[]{:S(2)}) async-start(), calls=%async_computation | async-start | bytes 11534336 | tf_op jit(solution)/shard_map/psum | solution.py:155
  164.4 409.5 %all-gather.7.cloned.1.call-start = ((), (), s32[]{:S(2)}) async-start(), calls=%async_computation.3 | async-start | bytes 4456448 | tf_op jit(solution)/shard_map/all_gather | solution.py:191
  166.2 295.7 %copy-start.82 = (pred[2]{0:T(512)(128)(4,1)}, pred[2]{0:T(512)(128)(4,1)S(1)}, u32[]{:S(2)}) copy-start(pred[2]{0:T(512)(128)(4,1)S(1)} %get-tuple-element.172) | copy-start | bytes 10
  417.3 32.2 %slice-start.3 = ((s8[5767168]{0:T(1024)(128)(4,1)}), s8[1572864]{0:T(1024)(128)(4,1)S(1)}, s32[]{:S(2)}) async-start(s8[5767168]{0:T(1024)(128)(4,1)} %bitcast.706), calls=%async_computation.9 | async-start | bytes 3145728
  436.3 6.1 copy-start.106
  439.5 10.1 slice-start.4
  461.7 9.2 copy-start.6
  463.6 9.6 copy-start.33
  464.4 200.1 %all-reduce.15.cloned.1.call-start = ((), (), s32[]{:S(2)}) async-start(), calls=%async_computation.4 | async-start | bytes 3145728 | tf_op jit(solution)/shard_map/psum | solution.py:15
  577.7 96.6 %copy-start.38 = (bf16[2,1,192,1024]{3,2,0,1:T(8,128)(2,1)}, bf16[2,1,192,1024]{3,2,0,1:T(8,128)(2,1)S(1)}, u32[]{:S(2)}) copy-start(bf16[2,1,192,1024]{3,2,0,1:T(8,128)(2,1)S(1)} %get-tuple-element.52) | copy-start | bytes 2359300
  577.7 355.8 %all-reduce.13.cloned.1.call-start = ((), (), s32[]{:S(2)}) async-start(), calls=%async_computation.1 | async-start | bytes 11534336 | tf_op jit(solution)/shard_map/psum | solution.py:155
  945.7 39.0 %slice-start = ((s8[5767168]{0:T(1024)(128)(4,1)}), s8[1572864]{0:T(1024)(128)(4,1)S(1)}, s32[]{:S(2)}) async-start(s8[5767168]{0:T(1024)(128)(4,1)} %bitcast.704), calls=%async_computation.6 | async-start | bytes 3145728
  971.3 6.1 copy-start.105
  974.5 10.1 slice-start.1
  1045.6 32.5 %copy-start.35 = (f32[2,128,128]{1,2,0:T(8,128)}, f32[2,128,128]{1,2,0:T(8,128)S(1)}, u32[]{:S(2)}) copy-start(f32[2,128,128]{1,2,0:T(8,128)S(1)} %fusion.230) | copy-start | bytes 393220
  1050.0 15.5 %copy-start.80 = (pred[64,64]{1,0:T(8,128)(4,1)S(1)}, pred[64,64]{1,0:T(8,128)(4,1)}, u32[]{:S(2)}) copy-start(pred[64,64]{1,0:T(8,128)(4,1)} %iota_compare_fusion.60) | copy-start | bytes 12292
  1050.0 25.8 %copy-start.68 = (f32[64,64]{1,0:T(8,128)S(1)}, f32[64,64]{1,0:T(8,128)}, u32[]{:S(2)}) copy-start(f32[64,64]{1,0:T(8,128)} %fusion.377) | copy-start | bytes 49156
  1050.0 26.1 %copy-start.53 = (f32[2,192,192]{1,2,0:T(8,128)S(1)}, f32[2,192,192]{1,2,0:T(8,128)}, u32[]{:S(2)}) copy-start(f32[2,192,192]{1,2,0:T(8,128)} %copy-done.52) | copy-start | bytes 884740
  1052.2 25.5 %copy-start.74 = (f32[2,64,128]{2,1,0:T(8,128)S(1)}, f32[2,64,128]{2,1,0:T(8,128)}, u32[]{:S(2)}) copy-start(f32[2,64,128]{2,1,0:T(8,128)} %fusion.438) | copy-start | bytes 196612
  (64 other events, 165.2 us)
Sparse Core Ops, SparseCore 0:
  10.7 53.0 all-gather.4
  70.4 85.9 all-reduce.16
  164.5 240.8 all-reduce.10
  464.5 51.6 all-gather.6
  577.8 86.5 all-reduce.14
  672.7 260.7 all-reduce.12

commit v5 on v4

--- a/solution.py
+++ b/solution.py
@@ -68,6 +68,10 @@
     cross = -jnp.einsum("...ij,...jk->...ik", tail_inv, cross, precision=highest)
     top = jnp.concatenate([head_inv, jnp.zeros(gram.shape[:-2] + (width, rest), jnp.float32)], -1)
     return jnp.concatenate([top, jnp.concatenate([cross, tail_inv], -1)], -2)
+
+
+def skip_inverse(gram):
+    return jnp.broadcast_to(jnp.eye(gram.shape[-1], dtype=jnp.float32), gram.shape)
 
 
 def solve_packed(packed, raw_factors):
@@ -214,7 +218,19 @@
         )
         proj_own = jnp.einsum("abrx,asx->abrs", range_y, row_u, preferred_element_type=jnp.float32)
         proj_c = jnp.einsum("abrs,abst->abrt", proj_own, coupling, precision=highest)
-        gram_inv = factor_inverse(gram_matrix)
+        update_live = (row_tile[:, None] > col_tile[None, :]) & (col_tile[None, :] > panel_index)
+        inv_parts = []
+        for slot in range(tiles_row):
+            for cslot in range(tiles_col):
+                inv_parts.append(
+                    lax.cond(
+                        update_live[slot, cslot],
+                        factor_inverse,
+                        skip_inverse,
+                        gram_matrix[slot, cslot],
+                    )
+                )
+        gram_inv = jnp.stack(inv_parts).reshape(gram_matrix.shape)
         both = jnp.concatenate([proj_u, proj_c], axis=-1)
         middle = jnp.einsum("abrs,abst->abrt", gram_inv, both, precision=highest)
         cores = jnp.einsum("absr,abst->abrt", gram_inv, middle, precision=highest)

time: 1100 us -> 1110 us (level)
  waiting for transfers between devices: 696 us -> 654 us
  matrix products: 81.8 us -> 102 us
  local copies, waits for them, and re-layouts: 83.2 us -> 99.5 us
  other arithmetic: 205 us -> 221 us
    psum x2, waiting for transfers between devices: 496 us -> 454 us  [on_device(): lax.psum(jnp.concatenate([own_chol, relay.reshape(-1, tile_order)], axis=...]
    dot_general x2, matrix products: 1.1 us -> 14.2 us  [on_device(): jnp.einsum('abrs,asx->abrx', sketch_c, row_u, preferred_element_type=jnp....]
    another operation x5 -> x8, other arithmetic: 23.1 us -> 27.6 us  [factor_inverse(): lax.linalg.triangular_solve(tail, eye_rest, left_side=True, lower=True)]
    another operation x5 -> x8, other arithmetic: 43.9 us -> 47.4 us  [factor_inverse(): lax.linalg.triangular_solve(head, eye, left_side=True, lower=True)]
    another operation x7 -> x12, other arithmetic: 50.9 us -> 54.1 us  [factor_inverse(): lax.linalg.cholesky(gram[..., :width, :width], symmetrize_input=False)]
    another operation x7 -> x12, other arithmetic: 27.3 us -> 30.3 us  [factor_inverse(): tail = jnp.tril(lax.linalg.cholesky(tail, symmetrize_input=False))]
    unnamed x174 -> x138, local copies, waits for them, and re-layouts: 25.8 us -> 25.5 us
  transfers between devices with their start and end apart: 6 -> 6, of which waited for: 5 -> 5; matrix products, arithmetic and copies ran while one was open for 12% -> 15% of each run, Pallas kernels for 0% -> 0%
where the time goes in v5:
time: 1110 us
  waiting for transfers between devices  654 us (59%)
  other arithmetic  221 us (20%)
  matrix products  102 us (9%)
  local copies, waits for them, and re-layouts  99.5 us (9%)
  between operations  18.1 us (2%)
  loops' own time  13.5 us (1%)
    psum x2, waiting for transfers between devices, on_device(): lax.psum(jnp.concatenate([own_chol, relay.reshape(-1, tile_order)], axis=...  454 us
    psum x2, waiting for transfers between devices, broadcast(): return lax.psum(jnp.where(mine, shard, jnp.zeros_like(shard)), axis)  148 us
    another operation x12, other arithmetic, factor_inverse(): lax.linalg.cholesky(gram[..., :width, :width], symmetrize_input=False)  54.1 us
    all_gather x1, waiting for transfers between devices, on_device(): whole_tile = lax.all_gather(diagonal[diag_slot], 'col', axis=0, tiled=True)  50.7 us
    another operation x8, other arithmetic, factor_inverse(): lax.linalg.triangular_solve(head, eye, left_side=True, lower=True)  47.4 us
    another operation x12, other arithmetic, factor_inverse(): tail = jnp.tril(lax.linalg.cholesky(tail, symmetrize_input=False))  30.3 us
    gather x16, local copies, waits for them, and re-layouts, solve_packed(): inverse = jnp.tril(block.T, -1) + jnp.diag(1.0 / jnp.diagonal(block))  29 us
    another operation x8, other arithmetic, factor_inverse(): lax.linalg.triangular_solve(tail, eye_rest, left_side=True, lower=True)  27.6 us
  transfers between devices with their start and end apart: 6, of which 5 were waited for; matrix products, arithmetic and copies ran while one was open for 15% of the time, Pallas kernels for 0%

profile of v5, /device:TPU:37, one launch (start us, length us, event | category | flops | bytes accessed | tf_op | source)
XLA Modules:
  0.0 1107.4 jit_solution(877046258120083063)
XLA Ops:
  13.1 50.7 %all-gather.5.cloned.1.call-done = f32[1,1024,1024]{2,0,1:T(1,128)} async-done(((f32[1,64,1024]{2,0,1:T(1,128)}), f32[1,1024,1024]{2,0,1:T(1,128)}) %all-gather.5.cloned.1.call-update) | async-done | bytes 4194320 | tf_op jit(solution)/shard_map/all_gather | solution.py:135
  70.3 11.7 %conditional.6 = (f32[1024,1024]{1,0:T(8,128)}) conditional(s32[]{:T(128)} %convert_element_type.241, () %tuple.59, f32[1024,1024]{1,0:T(8,128)} %bitcast.697), branch_computations={%region_2.3_spmd, %region_3.8_spmd} | conditional | flops 2323448576 | bytes 115020296 | solution.py:153
  84.8 71.6 %all-reduce.19.cloned.1.call-done = (bf16[2,192,1024]{2,1,0:T(8,128)(2,1)}, bf16[2,192,1024]{2,1,0:T(8,128)(2,1)}) async-done(((bf16[2,192,1024]{2,1,0:T(8,128)(2,1)}, bf16[2,192,1024]{2,1,0:T(8,128)(2,1)}), (bf16[2,192,1024]{2,1,0:T(8,128)(2,1)}, bf16[2,192,1024]{2,1,0:T(8,128)(2,1)})) %all-reduce.19.cloned.1.call-update) | async-done | bytes 1572880 | tf_op jit(solution)/shard_map/psum | solution.py:15
  166.2 259.1 %all-reduce.13.cloned.1.call-done = f32[1408,1024]{1,0:T(8,128)} async-done(((f32[1408,1024]{1,0:T(8,128)}), f32[1408,1024]{1,0:T(8,128)}) %all-reduce.13.cloned.1.call-update) | async-done | bytes 5767184 | tf_op jit(solution)/shard_map/psum | solution.py:159
  490.4 63.3 %conditional.7 = (f32[1,192,192]{2,1,0:T(8,128)}) conditional(s32[]{:T(128)} %bitcast.96, () %tuple.60, f32[2,192,192]{1,2,0:T(8,128)} %copy.247), branch_computations={%region_7.10_spmd, %region_8.15_spmd} | conditional | flops 66474176 | bytes 3753568 | solution.py:226
  496.1 13.2 %custom-call.104 = f32[128,128]{1,0:T(8,128)} custom-call(f32[128,128]{1,0:T(8,128)} %slice.581), custom_call_target="Cholesky" | custom-call | tf_op jit(solution)/shard_map/cond/branch_1_fun/cholesky/custom-call.1 | solution.py:57
  512.9 11.3 %custom-call.105 = f32[1,128,128]{1,2,0:T(8,128)} custom-call(f32[1,128,128]{2,1,0:T(8,128)} %fusion.55), custom_call_target="InvertDiagBlocksLowerTriangular" | custom-call | tf_op jit(solution)/shard_map/cond/branch_1_fun/triangular_solve/custom-call.2 | solution.py:58
  529.0 7.2 custom-call.106
  539.6 6.3 custom-call.107
  553.7 63.9 %conditional.8 = (f32[1,192,192]{2,1,0:T(8,128)}) conditional(s32[]{:T(128)} %bitcast.109, () %tuple.61, f32[2,192,192]{1,2,0:T(8,128)} %copy.247), branch_computations={%region_11.16_spmd, %region_12.17_spmd} | conditional | flops 66474176 | bytes 3753568 | solution.py:226
  559.7 13.2 %custom-call.108 = f32[128,128]{1,0:T(8,128)} custom-call(f32[128,128]{1,0:T(8,128)} %slice.605), custom_call_target="Cholesky" | custom-call | tf_op jit(solution)/shard_map/cond/branch_1_fun/cholesky/custom-call.1 | solution.py:57
  576.4 11.3 %custom-call.109 = f32[1,128,128]{1,2,0:T(8,128)} custom-call(f32[1,128,128]{2,1,0:T(8,128)} %fusion.118), custom_call_target="InvertDiagBlocksLowerTriangular" | custom-call | tf_op jit(solution)/shard_map/cond/branch_1_fun/triangular_solve/custom-call.2 | solution.py:58
  592.5 7.2 custom-call.110
  603.2 6.3 custom-call.111
  637.6 76.8 %all-reduce.17.cloned.1.call-done = (bf16[2,192,1024]{2,1,0:T(8,128)(2,1)}, bf16[2,192,1024]{2,1,0:T(8,128)(2,1)}) async-done(((bf16[2,192,1024]{2,1,0:T(8,128)(2,1)}, bf16[2,192,1024]{2,1,0:T(8,128)(2,1)}), (bf16[2,192,1024]{2,1,0:T(8,128)(2,1)}, bf16[2,192,1024]{2,1,0:T(8,128)(2,1)})) %all-reduce.17.cloned.1.call-update) | async-done | bytes 1572880 | tf_op jit(solution)/shard_map/psum | solution.py:15
  727.9 195.2 %all-reduce.15.cloned.1.call-done = f32[1408,1024]{1,0:T(8,128)} async-done(((f32[1408,1024]{1,0:T(8,128)}), f32[1408,1024]{1,0:T(8,128)}) %all-reduce.15.cloned.1.call-update) | async-done | bytes 5767184 | tf_op jit(solution)/shard_map/psum | solution.py:159
  985.9 13.8 %select_convert_fusion = bf16[2,192,1024]{2,1,0:T(8,128)(2,1)S(1)} fusion(f32[2,192,1024]{2,1,0:T(8,128)S(1)} %copy-done.13, bf16[2,192,192]{1,2,0:T(8,128)(2,1)S(1)} %fusion.195, bf16[2,192,1024]{2,1,0:T(8,128)(2,1)S(1)} %broadcast_select_fusion.2, pred[2,192]{1,0:T(4,128)(4,1)S(1)} %iota_compare_fusion.81), kind=kOutput, calls=%fused_computation.361 | convolution fusion | flops 152174592 | bytes 3293568 | tf_op jit(solution)/shard_map/abrs,asx->abrx/dot_general | solution.py:207
  1006.1 39.8 %conditional.10 = (f32[1,192,192]{2,1,0:T(8,128)S(1)}) conditional(s32[]{:T(128)} %bitcast.153, () %tuple.64, f32[2,192,192]{1,2,0:T(8,128)S(1)} %copy.257), branch_computations={%region_18.23_spmd, %region_19.24_spmd} | conditional | flops 66474176 | bytes 3360296 | solution.py:226
  1006.4 11.7 %custom-call.128 = f32[128,128]{1,0:T(8,128)S(1)} custom-call(f32[128,128]{1,0:T(8,128)S(1)} %slice.608), custom_call_target="Cholesky" | custom-call | tf_op jit(solution)/shard_map/cond/branch_1_fun/cholesky/custom-call.1 | solution.py:57
  1019.3 9.8 custom-call.129
  1031.3 5.8 custom-call.130
  1047.5 42.2 %conditional.11 = (f32[1,192,192]{2,1,0:T(8,128)S(1)}) conditional(s32[]{:T(128)} %bitcast.154, () %tuple.65, f32[2,192,192]{1,2,0:T(8,128)S(1)} %copy.257), branch_computations={%region_20.25_spmd, %region_21.26_spmd} | conditional | flops 66474176 | bytes 3360296 | solution.py:226
  1051.6 11.7 %custom-call.132 = f32[128,128]{1,0:T(8,128)S(1)} custom-call(f32[128,128]{1,0:T(8,128)S(1)} %slice.611), custom_call_target="Cholesky" | custom-call | tf_op jit(solution)/shard_map/cond/branch_1_fun/cholesky/custom-call.1 | solution.py:57
  1064.5 9.8 custom-call.133
  (407 shorter events, 289.4 us)
Async XLA Ops:
  7.2 472.6 %copy-start = (bf16[192,1024]{1,0:T(8,128)(2,1)S(1)}, bf16[192,1024]{1,0:T(8,128)(2,1)}, u32[]{:S(2)}) copy-start(bf16[192,1024]{1,0:T(8,128)(2,1)} %param.26) | copy-start | bytes 1179652
  7.2 56.6 %all-gather.5.cloned.1.call-start = ((), (), s32[]{:S(2)}) async-start(), calls=%async_computation.2 | async-start | bytes 4456448 | tf_op jit(solution)/shard_map/all_gather | solution.py:135
  9.2 147.1 %all-reduce.19.cloned.1.call-start = ((), (), s32[]{:S(2)}) async-start(), calls=%async_computation.5 | async-start | bytes 3145728 | tf_op jit(solution)/shard_map/psum | solution.py:15
  70.2 355.1 %all-reduce.13.cloned.1.call-start = ((), (), s32[]{:S(2)}) async-start(), calls=%async_computation | async-start | bytes 11534336 | tf_op jit(solution)/shard_map/psum | solution.py:159
  164.3 461.2 %all-gather.7.cloned.1.call-start = ((), (), s32[]{:S(2)}) async-start(), calls=%async_computation.3 | async-start | bytes 4456448 | tf_op jit(solution)/shard_map/all_gather | solution.py:195
  166.2 262.4 %copy-start.43 = (bf16[2,192,1024]{2,1,0:T(8,128)(2,1)S(1)}, bf16[2,192,1024]{2,1,0:T(8,128)(2,1)}, u32[]{:S(2)}) copy-start(bf16[2,192,1024]{2,1,0:T(8,128)(2,1)} %get-tuple-element.75) | copy-start | bytes 2359300
  448.0 14.8 %slice-start.3 = ((s8[5767168]{0:T(1024)(128)(4,1)}), s8[4194304]{0:T(1024)(128)(4,1)S(1)}, s32[]{:S(2)}) async-start(s8[5767168]{0:T(1024)(128)(4,1)} %bitcast.700), calls=%async_computation.9 | async-start | bytes 8388608
  455.2 7.6 slice-start.4
  473.1 5.3 copy-start.86
  473.1 5.9 copy-start.84
  474.8 7.2 copy-start.25
  475.7 238.8 %all-reduce.17.cloned.1.call-start = ((), (), s32[]{:S(2)}) async-start(), calls=%async_computation.4 | async-start | bytes 3145728 | tf_op jit(solution)/shard_map/psum | solution.py:15
  482.0 4.9 copy-start.14
  482.0 4.9 copy-start.89
  629.2 96.3 %copy-start.27 = (bf16[2,1,192,1024]{3,2,0,1:T(8,128)(2,1)}, bf16[2,1,192,1024]{3,2,0,1:T(8,128)(2,1)S(1)}, u32[]{:S(2)}) copy-start(bf16[2,1,192,1024]{3,2,0,1:T(8,128)(2,1)S(1)} %get-tuple-element.79) | copy-start | bytes 2359300
  629.2 293.9 %all-reduce.15.cloned.1.call-start = ((), (), s32[]{:S(2)}) async-start(), calls=%async_computation.1 | async-start | bytes 11534336 | tf_op jit(solution)/shard_map/psum | solution.py:159
  722.4 5.3 copy-start.19
  923.1 5.3 copy-start.1
  935.5 39.0 %slice-start = ((s8[5767168]{0:T(1024)(128)(4,1)}), s8[1572864]{0:T(1024)(128)(4,1)S(1)}, s32[]{:S(2)}) async-start(s8[5767168]{0:T(1024)(128)(4,1)} %bitcast.698), calls=%async_computation.6 | async-start | bytes 3145728
  960.3 5.1 copy-start.10
  960.3 5.1 copy-start.11
  961.1 6.1 copy-start.96
  964.3 10.2 slice-start.1
  1006.3 13.0 %copy-start.64 = (f32[192,192]{1,0:T(8,128)}, f32[192,192]{1,0:T(8,128)S(1)}, u32[]{:S(2)}) copy-start(f32[192,192]{1,0:T(8,128)S(1)} %fusion.131) | copy-start | bytes 442372 | tf_op jit(solution)/shard_map/cond
  (53 other events, 110.2 us)
Sparse Core Ops, SparseCore 0:
  10.7 53.0 all-gather.4
  70.3 85.9 all-reduce.18
  164.4 260.7 all-reduce.12
  475.8 51.7 all-gather.6
  629.3 85.1 all-reduce.16
  722.5 200.5 all-reduce.14

commit v6 on v4

--- a/solution.py
+++ b/solution.py
@@ -75,17 +75,16 @@
     width = min(BLOCK, order)
     count = order // width
     lead = raw_factors.shape[:-1]
-    rows = raw_factors.reshape(-1, order).astype(jnp.float32)
+    rest = raw_factors.reshape(-1, order).astype(jnp.float32)
     done = []
     for step in range(count):
         lo, hi = step * width, (step + 1) * width
         block = packed[lo:hi, lo:hi]
         inverse = jnp.tril(block.T, -1) + jnp.diag(1.0 / jnp.diagonal(block))
-        rhs = rows[:, lo:hi]
-        if step:
-            prior = jnp.concatenate(done, axis=1)
-            rhs = rhs - jnp.dot(prior, packed[lo:hi, :lo].T, precision=fine)
-        done.append(jnp.dot(rhs, inverse.T, precision=fine))
+        part = jnp.dot(rest[:, :width], inverse.T, precision=fine)
+        done.append(part)
+        if step < count - 1:
+            rest = rest[:, width:] - jnp.dot(part, packed[hi:, lo:hi].T, precision=fine)
     return jnp.concatenate(done, axis=1).reshape(lead + (order,)).astype(jnp.bfloat16)
 
 

time: 1100 us -> 1070 us (0.973)
  local copies, waits for them, and re-layouts: 83.2 us -> 58.1 us
  matrix products: 81.8 us -> 68.3 us
    unnamed x174 -> x138, local copies, waits for them, and re-layouts: 25.8 us -> 10.6 us
    dot_general x30, matrix products: 35.7 us -> 22.3 us  [the longest x14 14.1 us: solve_packed(): rest = rest[:, width:] - jnp.dot(part, packed[hi:, lo:hi].T, precision=fine)]
where the time goes in v6:
time: 1070 us; the launch traced here: 1060 us
  waiting for transfers between devices  704 us (66%)
  other arithmetic  201 us (19%)
  matrix products  68.3 us (6%)
  local copies, waits for them, and re-layouts  58.1 us (5%)
  between operations  15.8 us (1%)
  loops' own time  11.5 us (1%)
    psum x2, waiting for transfers between devices, on_device(): lax.psum(jnp.concatenate([own_chol, relay.reshape(-1, tile_order)], axis=...  503 us
    psum x2, waiting for transfers between devices, broadcast(): return lax.psum(jnp.where(mine, shard, jnp.zeros_like(shard)), axis)  151 us
    another operation x7, other arithmetic, factor_inverse(): lax.linalg.cholesky(gram[..., :width, :width], symmetrize_input=False)  51.4 us
    all_gather x1, waiting for transfers between devices, on_device(): whole_tile = lax.all_gather(diagonal[diag_slot], 'col', axis=0, tiled=True)  50.7 us
    another operation x5, other arithmetic, factor_inverse(): lax.linalg.triangular_solve(head, eye, left_side=True, lower=True)  43.8 us
    another operation x7, other arithmetic, factor_inverse(): tail = jnp.tril(lax.linalg.cholesky(tail, symmetrize_input=False))  27.3 us
    gather x16, local copies, waits for them, and re-layouts, solve_packed(): inverse = jnp.tril(block.T, -1) + jnp.diag(1.0 / jnp.diagonal(block))  25.3 us
    another operation x5, other arithmetic, factor_inverse(): lax.linalg.triangular_solve(tail, eye_rest, left_side=True, lower=True)  23.2 us
  transfers between devices with their start and end apart: 6, of which 5 were waited for; matrix products, arithmetic and copies ran while one was open for 12% of the time, Pallas kernels for 0%

profile of v6, /device:TPU:37, one launch (start us, length us, event | category | flops | bytes accessed | tf_op | source)
XLA Modules:
  0.0 1059.7 jit_solution(13245202176100217547)
XLA Ops:
  13.1 50.7 %all-gather.5.cloned.1.call-done = f32[1,1024,1024]{2,0,1:T(1,128)} async-done(((f32[1,64,1024]{2,0,1:T(1,128)}), f32[1,1024,1024]{2,0,1:T(1,128)}) %all-gather.5.cloned.1.call-update) | async-done | bytes 4194320 | tf_op jit(solution)/shard_map/all_gather | solution.py:130
  63.8 5.1 copy.418
  70.3 11.3 %conditional.2 = (f32[1024,1024]{1,0:T(8,128)}) conditional(s32[]{:T(128)} %convert_element_type.169, () %tuple.29, f32[1024,1024]{1,0:T(8,128)} %bitcast.695), branch_computations={%region_2.3_spmd, %region_3.8_spmd} | conditional | flops 2323448576 | bytes 109777304 | solution.py:148
  81.6 2.8 broadcast_select_fusion.1
  84.3 72.0 %all-reduce.17.cloned.1.call-done = (bf16[2,192,1024]{2,1,0:T(8,128)(2,1)}, bf16[2,192,1024]{2,1,0:T(8,128)(2,1)}) async-done(((bf16[2,192,1024]{2,1,0:T(8,128)(2,1)}, bf16[2,192,1024]{2,1,0:T(8,128)(2,1)}), (bf16[2,192,1024]{2,1,0:T(8,128)(2,1)}, bf16[2,192,1024]{2,1,0:T(8,128)(2,1)})) %all-reduce.17.cloned.1.call-update) | async-done | bytes 1572880 | tf_op jit(solution)/shard_map/psum | solution.py:15
  158.6 5.9 pad_maximum_fusion
  166.3 245.0 %all-reduce.11.cloned.1.call-done = f32[1408,1024]{1,0:T(8,128)} async-done(((f32[1408,1024]{1,0:T(8,128)}), f32[1408,1024]{1,0:T(8,128)}) %all-reduce.11.cloned.1.call-update) | async-done | bytes 5767184 | tf_op jit(solution)/shard_map/psum | solution.py:154
  411.4 3.2 convert.64
  472.2 24.9 %custom-call.116 = f32[2,1,128,128]{3,2,1,0:T(8,128)} custom-call(f32[2,1,128,128]{3,2,1,0:T(8,128)} %slice.649), custom_call_target="Cholesky" | custom-call | tf_op jit(solution)/shard_map/cholesky/custom-call.0 | solution.py:57
  499.8 21.1 %custom-call.117 = f32[2,1,1,128,128]{3,4,2,1,0:T(8,128)} custom-call(f32[2,1,1,128,128]{4,3,2,1,0:T(8,128)} %fusion.227), custom_call_target="InvertDiagBlocksLowerTriangular" | custom-call | tf_op jit(solution)/shard_map/triangular_solve/custom-call.4 | solution.py:58
  526.1 13.1 %custom-call.118 = f32[2,1,64,64]{3,2,1,0:T(8,128)} custom-call(f32[2,1,64,64]{3,2,1,0:T(8,128)} %fusion.121), custom_call_target="Cholesky" | custom-call | tf_op jit(solution)/shard_map/cholesky/custom-call.2 | solution.py:64
  541.7 11.6 %custom-call.119 = f32[2,1,1,64,64]{3,4,2,1,0:T(8,128)} custom-call(f32[2,1,1,64,64]{4,3,2,1,0:T(8,128)} %fusion.261), custom_call_target="InvertDiagBlocksLowerTriangular" | custom-call | tf_op jit(solution)/shard_map/triangular_solve/custom-call.5 | solution.py:66
  562.0 3.8 bitcast_select_fusion.18
  565.8 5.3 conditional.3
  571.2 2.8 broadcast_select_fusion
  574.0 78.6 %all-reduce.15.cloned.1.call-done = (bf16[2,192,1024]{2,1,0:T(8,128)(2,1)}, bf16[2,192,1024]{2,1,0:T(8,128)(2,1)}) async-done(((bf16[2,192,1024]{2,1,0:T(8,128)(2,1)}, bf16[2,192,1024]{2,1,0:T(8,128)(2,1)}), (bf16[2,192,1024]{2,1,0:T(8,128)(2,1)}, bf16[2,192,1024]{2,1,0:T(8,128)(2,1)})) %all-reduce.15.cloned.1.call-update) | async-done | bytes 1572880 | tf_op jit(solution)/shard_map/psum | solution.py:15
  654.8 5.9 pad_maximum_fusion.1
  664.9 257.9 %all-reduce.13.cloned.1.call-done = f32[1408,1024]{1,0:T(8,128)} async-done(((f32[1408,1024]{1,0:T(8,128)}), f32[1408,1024]{1,0:T(8,128)}) %all-reduce.13.cloned.1.call-update) | async-done | bytes 5767184 | tf_op jit(solution)/shard_map/psum | solution.py:154
  922.8 3.2 convert.74
  939.2 2.6 gather_fusion.14
  964.8 23.9 %custom-call.120 = f32[2,1,128,128]{3,2,1,0:T(8,128)S(1)} custom-call(f32[2,1,128,128]{3,2,1,0:T(8,128)S(1)} %slice.687), custom_call_target="Cholesky" | custom-call | tf_op jit(solution)/shard_map/cholesky/custom-call.0 | solution.py:57
  990.5 19.7 %custom-call.121 = f32[2,1,1,128,128]{3,4,2,1,0:T(8,128)S(1)} custom-call(f32[2,1,1,128,128]{4,3,2,1,0:T(8,128)S(1)} %fusion.221), custom_call_target="InvertDiagBlocksLowerTriangular" | custom-call | tf_op jit(solution)/shard_map/triangular_solve/custom-call.4 | solution.py:58
  1018.6 12.5 %custom-call.122 = f32[2,1,64,64]{3,2,1,0:T(8,128)S(1)} custom-call(f32[2,1,64,64]{3,2,1,0:T(8,128)} %fusion.122), custom_call_target="Cholesky" | custom-call | tf_op jit(solution)/shard_map/cholesky/custom-call.2 | solution.py:64
  1031.3 10.0 custom-call.123
  (325 shorter events, 156.1 us)
Async XLA Ops:
  7.2 451.7 %copy-start = (bf16[192,1024]{1,0:T(8,128)(2,1)S(1)}, bf16[192,1024]{1,0:T(8,128)(2,1)}, u32[]{:S(2)}) copy-start(bf16[192,1024]{1,0:T(8,128)(2,1)} %param.21) | copy-start | bytes 1179652
  7.2 56.6 %all-gather.5.cloned.1.call-start = ((), (), s32[]{:S(2)}) async-start(), calls=%async_computation.2 | async-start | bytes 4456448 | tf_op jit(solution)/shard_map/all_gather | solution.py:130
  9.2 147.1 %all-reduce.17.cloned.1.call-start = ((), (), s32[]{:S(2)}) async-start(), calls=%async_computation.5 | async-start | bytes 3145728 | tf_op jit(solution)/shard_map/psum | solution.py:15
  11.5 57.4 %copy-start.66 = (pred[2,192]{1,0:T(4,128)(4,1)}, pred[2,192]{1,0:T(4,128)(4,1)S(1)}, u32[]{:S(2)}) copy-start(pred[2,192]{1,0:T(4,128)(4,1)S(1)} %compare_and_fusion) | copy-start | bytes 1156
  13.1 55.9 %copy-start.5 = (bf16[2,192,1024]{2,1,0:T(8,128)(2,1)}, bf16[2,192,1024]{2,1,0:T(8,128)(2,1)S(1)}, u32[]{:S(2)}) copy-start(bf16[2,192,1024]{2,1,0:T(8,128)(2,1)S(1)} %get-tuple-element.22) | copy-start | bytes 2359300
  70.2 341.1 %all-reduce.11.cloned.1.call-start = ((), (), s32[]{:S(2)}) async-start(), calls=%async_computation | async-start | bytes 11534336 | tf_op jit(solution)/shard_map/psum | solution.py:154
  164.5 397.4 %all-gather.7.cloned.1.call-start = ((), (), s32[]{:S(2)}) async-start(), calls=%async_computation.3 | async-start | bytes 4456448 | tf_op jit(solution)/shard_map/all_gather | solution.py:190
  166.2 283.5 %copy-start.67 = (pred[2]{0:T(512)(128)(4,1)}, pred[2]{0:T(512)(128)(4,1)S(1)}, u32[]{:S(2)}) copy-start(pred[2]{0:T(512)(128)(4,1)S(1)} %get-tuple-element.138) | copy-start | bytes 10
  166.3 248.3 %copy-start.41 = (bf16[2,192,1024]{2,1,0:T(8,128)(2,1)S(1)}, bf16[2,192,1024]{2,1,0:T(8,128)(2,1)}, u32[]{:S(2)}) copy-start(bf16[2,192,1024]{2,1,0:T(8,128)(2,1)} %get-tuple-element.48) | copy-start | bytes 2359300
  427.3 13.0 %slice-start.3 = ((s8[5767168]{0:T(1024)(128)(4,1)}), s8[1572864]{0:T(1024)(128)(4,1)S(1)}, s32[]{:S(2)}) async-start(s8[5767168]{0:T(1024)(128)(4,1)} %bitcast.698), calls=%async_computation.9 | async-start | bytes 3145728
  449.6 9.3 copy-start.6
  451.4 11.2 %copy-start.27 = (f32[2,64,1024]{2,1,0:T(8,128)}, f32[2,64,1024]{2,1,0:T(8,128)S(1)}, u32[]{:S(2)}) copy-start(f32[2,64,1024]{2,1,0:T(8,128)S(1)} %fusion.107) | copy-start | bytes 1572868
  452.2 10.4 copy-start.68
  452.2 200.4 %all-reduce.15.cloned.1.call-start = ((), (), s32[]{:S(2)}) async-start(), calls=%async_computation.4 | async-start | bytes 3145728 | tf_op jit(solution)/shard_map/psum | solution.py:15
  565.8 96.7 %copy-start.33 = (bf16[2,1,192,1024]{3,2,0,1:T(8,128)(2,1)}, bf16[2,1,192,1024]{3,2,0,1:T(8,128)(2,1)S(1)}, u32[]{:S(2)}) copy-start(bf16[2,1,192,1024]{3,2,0,1:T(8,128)(2,1)S(1)} %get-tuple-element.52) | copy-start | bytes 2359300
  565.8 357.0 %all-reduce.13.cloned.1.call-start = ((), (), s32[]{:S(2)}) async-start(), calls=%async_computation.1 | async-start | bytes 11534336 | tf_op jit(solution)/shard_map/psum | solution.py:154
  660.7 262.0 %copy-start.71 = (pred[2]{0:T(512)(128)(4,1)}, pred[2]{0:T(512)(128)(4,1)S(1)}, u32[]{:S(2)}) copy-start(pred[2]{0:T(512)(128)(4,1)S(1)} %broadcast_compare_fusion.1) | copy-start | bytes 10
  664.9 261.2 %copy-start.42 = (bf16[2,192,1024]{2,1,0:T(8,128)(2,1)S(1)}, bf16[2,192,1024]{2,1,0:T(8,128)(2,1)}, u32[]{:S(2)}) copy-start(bf16[2,192,1024]{2,1,0:T(8,128)(2,1)} %get-tuple-element.46) | copy-start | bytes 2359300
  939.2 13.8 %slice-start = ((s8[5767168]{0:T(1024)(128)(4,1)}), s8[1572864]{0:T(1024)(128)(4,1)S(1)}, s32[]{:S(2)}) async-start(s8[5767168]{0:T(1024)(128)(4,1)} %bitcast.696), calls=%async_computation.6 | async-start | bytes 3145728
  1015.6 15.5 %copy-start.65 = (pred[64,64]{1,0:T(8,128)(4,1)S(1)}, pred[64,64]{1,0:T(8,128)(4,1)}, u32[]{:S(2)}) copy-start(pred[64,64]{1,0:T(8,128)(4,1)} %iota_compare_fusion.60) | copy-start | bytes 12292
  1015.6 25.7 %copy-start.57 = (f32[64,64]{1,0:T(8,128)S(1)}, f32[64,64]{1,0:T(8,128)}, u32[]{:S(2)}) copy-start(f32[64,64]{1,0:T(8,128)} %fusion.347) | copy-start | bytes 49156
  1015.6 26.0 %copy-start.44 = (f32[2,192,192]{1,2,0:T(8,128)S(1)}, f32[2,192,192]{1,2,0:T(8,128)}, u32[]{:S(2)}) copy-start(f32[2,192,192]{1,2,0:T(8,128)} %copy-done.43) | copy-start | bytes 884740
  1043.2 5.8 copy-start.22
  1043.2 5.8 copy-start.73
  (52 other events, 139.5 us)
Sparse Core Ops, SparseCore 0:
  10.7 53.0 all-gather.4
  70.3 85.9 all-reduce.16
  164.6 246.6 all-reduce.10
  452.3 51.7 all-gather.6
  565.9 86.6 all-reduce.14
  660.8 261.8 all-reduce.12

commit v7 on v6

--- a/solution.py
+++ b/solution.py
@@ -34,19 +34,22 @@
     order = tile_mat.shape[0]
     width = min(BLOCK, order)
     count = order // width
-    work = (tile_mat + tile_mat.T) * 0.5
+    sym = (tile_mat + tile_mat.T) * 0.5
     eye = jnp.eye(width, dtype=jnp.float32)
-    strips = []
+    packed = jnp.zeros((order, order), jnp.float32)
     for step in range(count):
-        head = jnp.tril(lax.linalg.cholesky(work[:width, :width], symmetrize_input=False))
+        lo, hi = step * width, (step + 1) * width
+        column = sym[lo:, lo:hi]
+        if step:
+            column = column - jnp.dot(packed[lo:, :lo], packed[lo:hi, :lo].T, precision=fine)
+        head = jnp.tril(lax.linalg.cholesky(column[:width], symmetrize_input=False))
         head_inv = lax.linalg.triangular_solve(head, eye, left_side=True, lower=True)
-        parts = [jnp.zeros((step * width, width), jnp.float32), head + jnp.triu(head_inv.T, 1)]
+        block = head + jnp.triu(head_inv.T, 1)
         if step < count - 1:
-            below = jnp.dot(work[width:, :width], head_inv.T, precision=fine)
-            work = work[width:, width:] - jnp.dot(below, below.T, precision=fine)
-            parts.append(below)
-        strips.append(jnp.concatenate(parts, axis=0))
-    return jnp.concatenate(strips, axis=1)
+            below = jnp.dot(column[width:], head_inv.T, precision=fine)
+            block = jnp.concatenate([block, below], axis=0)
+        packed = lax.dynamic_update_slice(packed, block, (lo, lo))
+    return packed
 
 
 def factor_inverse(gram):

time: 1070 us -> 1010 us (0.944)
  waiting for transfers between devices: 704 us -> 638 us
    psum x2, waiting for transfers between devices: 503 us -> 436 us  [on_device(): lax.psum(jnp.concatenate([own_chol, relay.reshape(-1, tile_order)], axis=...]
  transfers between devices with their start and end apart: 6 -> 6, of which waited for: 5 -> 5; matrix products, arithmetic and copies ran while one was open for 12% -> 13% of each run, Pallas kernels for 0% -> 0%
where the time goes in v7:
time: 1010 us; the launch traced here: 1000 us
  waiting for transfers between devices  638 us (63%)
  other arithmetic  208 us (21%)
  matrix products  72.3 us (7%)
  local copies, waits for them, and re-layouts  58 us (6%)
  between operations  15.7 us (2%)
  loops' own time  11.5 us (1%)
    psum x2, waiting for transfers between devices, on_device(): lax.psum(jnp.concatenate([own_chol, relay.reshape(-1, tile_order)], axis=...  436 us
    psum x2, waiting for transfers between devices, broadcast(): return lax.psum(jnp.where(mine, shard, jnp.zeros_like(shard)), axis)  151 us
    another operation x7, other arithmetic, factor_inverse(): lax.linalg.cholesky(gram[..., :width, :width], symmetrize_input=False)  51.4 us
    all_gather x1, waiting for transfers between devices, on_device(): whole_tile = lax.all_gather(diagonal[diag_slot], 'col', axis=0, tiled=True)  50.7 us
    another operation x5, other arithmetic, factor_inverse(): lax.linalg.triangular_solve(head, eye, left_side=True, lower=True)  43.8 us
    another operation x7, other arithmetic, factor_inverse(): tail = jnp.tril(lax.linalg.cholesky(tail, symmetrize_input=False))  28.7 us
    another operation x5, other arithmetic, factor_inverse(): lax.linalg.triangular_solve(tail, eye_rest, left_side=True, lower=True)  26 us
    gather x16, local copies, waits for them, and re-layouts, solve_packed(): inverse = jnp.tril(block.T, -1) + jnp.diag(1.0 / jnp.diagonal(block))  25.4 us
  transfers between devices with their start and end apart: 6, of which 5 were waited for; matrix products, arithmetic and copies ran while one was open for 13% of the time, Pallas kernels for 0%

profile of v7, /device:TPU:37, one launch (start us, length us, event | category | flops | bytes accessed | tf_op | source)
XLA Modules:
  0.0 1004.0 jit_solution(10455094959408866507)
XLA Ops:
  13.2 50.7 %all-gather.5.cloned.1.call-done = f32[1,1024,1024]{2,0,1:T(1,128)} async-done(((f32[1,64,1024]{2,0,1:T(1,128)}), f32[1,1024,1024]{2,0,1:T(1,128)}) %all-gather.5.cloned.1.call-update) | async-done | bytes 4194320 | tf_op jit(solution)/shard_map/all_gather | solution.py:133
  63.8 5.1 copy.418
  70.3 11.2 %conditional.2 = (f32[1024,1024]{1,0:T(8,128)}) conditional(s32[]{:T(128)} %convert_element_type.169, () %tuple.29, f32[1024,1024]{1,0:T(8,128)} %bitcast.673), branch_computations={%region_2.3_spmd, %region_3.8_spmd} | conditional | flops 1619903488 | bytes 81994304 | solution.py:151
  81.5 2.8 broadcast_select_fusion.1
  84.3 72.2 %all-reduce.17.cloned.1.call-done = (bf16[2,192,1024]{2,1,0:T(8,128)(2,1)}, bf16[2,192,1024]{2,1,0:T(8,128)(2,1)}) async-done(((bf16[2,192,1024]{2,1,0:T(8,128)(2,1)}, bf16[2,192,1024]{2,1,0:T(8,128)(2,1)}), (bf16[2,192,1024]{2,1,0:T(8,128)(2,1)}, bf16[2,192,1024]{2,1,0:T(8,128)(2,1)})) %all-reduce.17.cloned.1.call-update) | async-done | bytes 1572880 | tf_op jit(solution)/shard_map/psum | solution.py:15
  158.7 5.9 pad_maximum_fusion
  166.6 218.4 %all-reduce.11.cloned.1.call-done = f32[1408,1024]{1,0:T(8,128)} async-done(((f32[1408,1024]{1,0:T(8,128)}), f32[1408,1024]{1,0:T(8,128)}) %all-reduce.11.cloned.1.call-update) | async-done | bytes 5767184 | tf_op jit(solution)/shard_map/psum | solution.py:157
  385.0 3.2 convert.64
  446.5 24.9 %custom-call.116 = f32[2,1,128,128]{3,2,1,0:T(8,128)} custom-call(f32[2,1,128,128]{3,2,1,0:T(8,128)} %slice.761), custom_call_target="Cholesky" | custom-call | tf_op jit(solution)/shard_map/cholesky/custom-call.0 | solution.py:60
  474.1 21.1 %custom-call.117 = f32[2,1,1,128,128]{3,4,2,1,0:T(8,128)} custom-call(f32[2,1,1,128,128]{4,3,2,1,0:T(8,128)} %fusion.253), custom_call_target="InvertDiagBlocksLowerTriangular" | custom-call | tf_op jit(solution)/shard_map/triangular_solve/custom-call.4 | solution.py:61
  500.4 13.1 %custom-call.118 = f32[2,1,64,64]{3,2,1,0:T(8,128)} custom-call(f32[2,1,64,64]{3,2,1,0:T(8,128)} %fusion.147), custom_call_target="Cholesky" | custom-call | tf_op jit(solution)/shard_map/cholesky/custom-call.2 | solution.py:67
  516.0 11.6 %custom-call.119 = f32[2,1,1,64,64]{3,4,2,1,0:T(8,128)} custom-call(f32[2,1,1,64,64]{4,3,2,1,0:T(8,128)} %fusion.287), custom_call_target="InvertDiagBlocksLowerTriangular" | custom-call | tf_op jit(solution)/shard_map/triangular_solve/custom-call.5 | solution.py:69
  537.3 3.8 bitcast_select_fusion.18
  541.2 5.3 conditional.3
  546.5 2.8 broadcast_select_fusion
  549.2 78.6 %all-reduce.15.cloned.1.call-done = (bf16[2,192,1024]{2,1,0:T(8,128)(2,1)}, bf16[2,192,1024]{2,1,0:T(8,128)(2,1)}) async-done(((bf16[2,192,1024]{2,1,0:T(8,128)(2,1)}, bf16[2,192,1024]{2,1,0:T(8,128)(2,1)}), (bf16[2,192,1024]{2,1,0:T(8,128)(2,1)}, bf16[2,192,1024]{2,1,0:T(8,128)(2,1)})) %all-reduce.15.cloned.1.call-update) | async-done | bytes 1572880 | tf_op jit(solution)/shard_map/psum | solution.py:15
  630.1 5.9 pad_maximum_fusion.1
  641.3 217.9 %all-reduce.13.cloned.1.call-done = f32[1408,1024]{1,0:T(8,128)} async-done(((f32[1408,1024]{1,0:T(8,128)}), f32[1408,1024]{1,0:T(8,128)}) %all-reduce.13.cloned.1.call-update) | async-done | bytes 5767184 | tf_op jit(solution)/shard_map/psum | solution.py:157
  859.2 3.2 convert.74
  875.7 2.6 gather_fusion.14
  901.4 23.9 %custom-call.120 = f32[2,1,128,128]{3,2,1,0:T(8,128)S(1)} custom-call(f32[2,1,128,128]{3,2,1,0:T(8,128)S(1)} %slice.799), custom_call_target="Cholesky" | custom-call | tf_op jit(solution)/shard_map/cholesky/custom-call.0 | solution.py:60
  927.0 19.7 %custom-call.121 = f32[2,1,1,128,128]{3,4,2,1,0:T(8,128)S(1)} custom-call(f32[2,1,1,128,128]{4,3,2,1,0:T(8,128)S(1)} %fusion.247), custom_call_target="InvertDiagBlocksLowerTriangular" | custom-call | tf_op jit(solution)/shard_map/triangular_solve/custom-call.4 | solution.py:61
  955.2 13.1 %custom-call.122 = f32[2,1,64,64]{3,2,1,0:T(8,128)} custom-call(f32[2,1,64,64]{3,2,1,0:T(8,128)} %fusion.148), custom_call_target="Cholesky" | custom-call | tf_op jit(solution)/shard_map/cholesky/custom-call.2 | solution.py:67
  970.8 11.3 %custom-call.123 = f32[2,1,1,64,64]{3,4,2,1,0:T(8,128)} custom-call(f32[2,1,1,64,64]{4,3,2,1,0:T(8,128)} %fusion.265), custom_call_target="InvertDiagBlocksLowerTriangular" | custom-call | tf_op jit(solution)/shard_map/triangular_solve/custom-call.5 | solution.py:69
  (311 shorter events, 165.1 us)
Async XLA Ops:
  7.2 426.0 %copy-start = (bf16[192,1024]{1,0:T(8,128)(2,1)S(1)}, bf16[192,1024]{1,0:T(8,128)(2,1)}, u32[]{:S(2)}) copy-start(bf16[192,1024]{1,0:T(8,128)(2,1)} %param.21) | copy-start | bytes 1179652
  7.2 56.6 %all-gather.5.cloned.1.call-start = ((), (), s32[]{:S(2)}) async-start(), calls=%async_computation.2 | async-start | bytes 4456448 | tf_op jit(solution)/shard_map/all_gather | solution.py:133
  9.2 147.2 %all-reduce.17.cloned.1.call-start = ((), (), s32[]{:S(2)}) async-start(), calls=%async_computation.5 | async-start | bytes 3145728 | tf_op jit(solution)/shard_map/psum | solution.py:15
  11.6 57.3 %copy-start.34 = (pred[2,192]{1,0:T(4,128)(4,1)}, pred[2,192]{1,0:T(4,128)(4,1)S(1)}, u32[]{:S(2)}) copy-start(pred[2,192]{1,0:T(4,128)(4,1)S(1)} %compare_and_fusion) | copy-start | bytes 1156
  13.1 55.8 %copy-start.5 = (bf16[2,192,1024]{2,1,0:T(8,128)(2,1)}, bf16[2,192,1024]{2,1,0:T(8,128)(2,1)S(1)}, u32[]{:S(2)}) copy-start(bf16[2,192,1024]{2,1,0:T(8,128)(2,1)S(1)} %get-tuple-element.22) | copy-start | bytes 2359300
  70.2 314.8 %all-reduce.11.cloned.1.call-start = ((), (), s32[]{:S(2)}) async-start(), calls=%async_computation | async-start | bytes 11534336 | tf_op jit(solution)/shard_map/psum | solution.py:157
  164.6 372.7 %all-gather.7.cloned.1.call-start = ((), (), s32[]{:S(2)}) async-start(), calls=%async_computation.3 | async-start | bytes 4456448 | tf_op jit(solution)/shard_map/all_gather | solution.py:193
  166.4 257.6 %copy-start.35 = (pred[2]{0:T(512)(128)(4,1)}, pred[2]{0:T(512)(128)(4,1)S(1)}, u32[]{:S(2)}) copy-start(pred[2]{0:T(512)(128)(4,1)S(1)} %get-tuple-element.138) | copy-start | bytes 10
  166.5 221.7 %copy-start.25 = (bf16[2,192,1024]{2,1,0:T(8,128)(2,1)S(1)}, bf16[2,192,1024]{2,1,0:T(8,128)(2,1)}, u32[]{:S(2)}) copy-start(bf16[2,192,1024]{2,1,0:T(8,128)(2,1)} %get-tuple-element.48) | copy-start | bytes 2359300
  401.0 13.6 %slice-start.3 = ((s8[5767168]{0:T(1024)(128)(4,1)}), s8[1572864]{0:T(1024)(128)(4,1)S(1)}, s32[]{:S(2)}) async-start(s8[5767168]{0:T(1024)(128)(4,1)} %bitcast.676), calls=%async_computation.9 | async-start | bytes 3145728
  423.9 9.3 copy-start.6
  425.7 12.9 %copy-start.16 = (f32[2,64,1024]{2,1,0:T(8,128)}, f32[2,64,1024]{2,1,0:T(8,128)S(1)}, u32[]{:S(2)}) copy-start(f32[2,64,1024]{2,1,0:T(8,128)S(1)} %fusion.133) | copy-start | bytes 1572868
  425.7 11.1 %copy-start.36 = (pred[2]{0:T(512)(128)(4,1)S(1)}, pred[2]{0:T(512)(128)(4,1)}, u32[]{:S(2)}) copy-start(pred[2]{0:T(512)(128)(4,1)} %copy-done.35) | copy-start | bytes 10
  426.6 201.3 %all-reduce.15.cloned.1.call-start = ((), (), s32[]{:S(2)}) async-start(), calls=%async_computation.4 | async-start | bytes 3145728 | tf_op jit(solution)/shard_map/psum | solution.py:15
  541.1 97.2 %copy-start.20 = (bf16[2,1,192,1024]{3,2,0,1:T(8,128)(2,1)}, bf16[2,1,192,1024]{3,2,0,1:T(8,128)(2,1)S(1)}, u32[]{:S(2)}) copy-start(bf16[2,1,192,1024]{3,2,0,1:T(8,128)(2,1)S(1)} %get-tuple-element.52) | copy-start | bytes 2359300
  541.1 318.1 %all-reduce.13.cloned.1.call-start = ((), (), s32[]{:S(2)}) async-start(), calls=%async_computation.1 | async-start | bytes 11534336 | tf_op jit(solution)/shard_map/psum | solution.py:157
  641.2 221.2 %copy-start.26 = (bf16[2,192,1024]{2,1,0:T(8,128)(2,1)S(1)}, bf16[2,192,1024]{2,1,0:T(8,128)(2,1)}, u32[]{:S(2)}) copy-start(bf16[2,192,1024]{2,1,0:T(8,128)(2,1)} %get-tuple-element.46) | copy-start | bytes 2359300
  875.7 13.8 %slice-start = ((s8[5767168]{0:T(1024)(128)(4,1)}), s8[1572864]{0:T(1024)(128)(4,1)S(1)}, s32[]{:S(2)}) async-start(s8[5767168]{0:T(1024)(128)(4,1)} %bitcast.674), calls=%async_computation.6 | async-start | bytes 3145728
  954.4 37.1 %copy-start.13 = (bf16[2,192,1024]{2,1,0:T(8,128)(2,1)S(1)}, bf16[2,192,1024]{2,1,0:T(8,128)(2,1)}, u32[]{:S(2)}) copy-start(bf16[2,192,1024]{2,1,0:T(8,128)(2,1)} %get-tuple-element.45) | copy-start | bytes 2359300
  954.4 37.1 %copy-start.40 = (pred[2]{0:T(512)(128)(4,1)S(1)}, pred[2]{0:T(512)(128)(4,1)}, u32[]{:S(2)}) copy-start(pred[2]{0:T(512)(128)(4,1)} %broadcast_compare_fusion.1) | copy-start | bytes 10
  954.4 37.1 %copy-start.41 = (pred[2]{0:T(512)(128)(4,1)S(1)}, pred[2]{0:T(512)(128)(4,1)}, u32[]{:S(2)}) copy-start(pred[2]{0:T(512)(128)(4,1)} %get-tuple-element.49) | copy-start | bytes 10
  985.0 8.3 copy-start.21
  985.0 8.3 copy-start.32
  985.0 8.3 copy-start.48
  (45 other events, 141.2 us)
Sparse Core Ops, SparseCore 0:
  10.7 53.0 all-gather.4
  70.3 86.0 all-reduce.16
  164.7 220.1 all-reduce.10
  426.7 51.8 all-gather.6
  541.2 86.5 all-reduce.14
  636.1 222.9 all-reduce.12

commit v8 on v7

--- a/solution.py
+++ b/solution.py
@@ -62,13 +62,13 @@
     if width == order:
         return head_inv
     rest = order - width
-    below = jnp.einsum("...ij,...kj->...ik", gram[..., width:, :width], head_inv, precision=highest)
-    tail = gram[..., width:, width:] - jnp.einsum("...ij,...kj->...ik", below, below, precision=highest)
+    below = jnp.einsum("...ij,...kj->...ik", gram[..., width:, :width], head_inv, precision=fine)
+    tail = gram[..., width:, width:] - jnp.einsum("...ij,...kj->...ik", below, below, precision=fine)
     tail = jnp.tril(lax.linalg.cholesky(tail, symmetrize_input=False))
     eye_rest = jnp.broadcast_to(jnp.eye(rest, dtype=jnp.float32), gram.shape[:-2] + (rest, rest))
     tail_inv = lax.linalg.triangular_solve(tail, eye_rest, left_side=True, lower=True)
-    cross = jnp.einsum("...ij,...jk->...ik", below, head_inv, precision=highest)
-    cross = -jnp.einsum("...ij,...jk->...ik", tail_inv, cross, precision=highest)
+    cross = jnp.einsum("...ij,...jk->...ik", below, head_inv, precision=fine)
+    cross = -jnp.einsum("...ij,...jk->...ik", tail_inv, cross, precision=fine)
     top = jnp.concatenate([head_inv, jnp.zeros(gram.shape[:-2] + (width, rest), jnp.float32)], -1)
     return jnp.concatenate([top, jnp.concatenate([cross, tail_inv], -1)], -2)
 
@@ -196,7 +196,7 @@
         sketch_v = jnp.einsum(
             "rx,absx->abrs", sketch, factor_v, preferred_element_type=jnp.float32
         ).astype(jnp.bfloat16)
-        sketch_c = jnp.einsum("brs,abts->abrt", col_sketch, coupling, precision=highest).astype(
+        sketch_c = jnp.einsum("brs,abts->abrt", col_sketch, coupling, precision=fine).astype(
             jnp.bfloat16
         )
         range_y = jnp.einsum(
@@ -215,11 +215,11 @@
             "abrx,absx->abrs", range_y, factor_u, preferred_element_type=jnp.float32
         )
         proj_own = jnp.einsum("abrx,asx->abrs", range_y, row_u, preferred_element_type=jnp.float32)
-        proj_c = jnp.einsum("abrs,abst->abrt", proj_own, coupling, precision=highest)
+        proj_c = jnp.einsum("abrs,abst->abrt", proj_own, coupling, precision=fine)
         gram_inv = factor_inverse(gram_matrix)
         both = jnp.concatenate([proj_u, proj_c], axis=-1)
-        middle = jnp.einsum("abrs,abst->abrt", gram_inv, both, precision=highest)
-        cores = jnp.einsum("absr,abst->abrt", gram_inv, middle, precision=highest)
+        middle = jnp.einsum("abrs,abst->abrt", gram_inv, both, precision=fine)
+        cores = jnp.einsum("absr,abst->abrt", gram_inv, middle, precision=fine)
         first_core = cores[..., :rank_width].astype(jnp.bfloat16)
         second_core = cores[..., rank_width:].astype(jnp.bfloat16)
         fresh_v = jnp.einsum(

time: 1010 us -> 1020 us (level)
  starting transfers between devices: 0.46 us -> 11 us
    psum x2, starting transfers between devices: 0.3 us -> 10.8 us  [broadcast(): return lax.psum(jnp.where(mine, shard, jnp.zeros_like(shard)), axis)]
where the time goes in v8:
time: 1020 us; the launch traced here: 1010 us
  waiting for transfers between devices  629 us (62%)
  other arithmetic  207 us (20%)
  matrix products  69.2 us (7%)
  local copies, waits for them, and re-layouts  58.1 us (6%)
  loops' own time  20 us (2%)
  between operations  15.7 us (2%)
  starting transfers between devices  11 us (1%)
    psum x2, waiting for transfers between devices, on_device(): lax.psum(jnp.concatenate([own_chol, relay.reshape(-1, tile_order)], axis=...  436 us
    psum x2, waiting for transfers between devices, broadcast(): return lax.psum(jnp.where(mine, shard, jnp.zeros_like(shard)), axis)  142 us
    another operation x7, other arithmetic, factor_inverse(): lax.linalg.cholesky(gram[..., :width, :width], symmetrize_input=False)  51.1 us
    all_gather x1, waiting for transfers between devices, on_device(): whole_tile = lax.all_gather(diagonal[diag_slot], 'col', axis=0, tiled=True)  50.7 us
    another operation x5, other arithmetic, factor_inverse(): lax.linalg.triangular_solve(head, eye, left_side=True, lower=True)  43.8 us
    another operation x7, other arithmetic, factor_inverse(): tail = jnp.tril(lax.linalg.cholesky(tail, symmetrize_input=False))  28.7 us
    gather x16, local copies, waits for them, and re-layouts, solve_packed(): inverse = jnp.tril(block.T, -1) + jnp.diag(1.0 / jnp.diagonal(block))  25.5 us
    another operation x5, other arithmetic, factor_inverse(): lax.linalg.triangular_solve(tail, eye_rest, left_side=True, lower=True)  25.5 us
  transfers between devices with their start and end apart: 6, of which 5 were waited for; matrix products, arithmetic and copies ran while one was open for 13% of the time, Pallas kernels for 0%

profile of v8, /device:TPU:37, one launch (start us, length us, event | category | flops | bytes accessed | tf_op | source)
XLA Modules:
  0.0 1010.9 jit_solution(12940567317584229550)
XLA Ops:
  13.2 50.7 %all-gather.5.cloned.1.call-done = f32[1,1024,1024]{2,0,1:T(1,128)} async-done(((f32[1,64,1024]{2,0,1:T(1,128)}), f32[1,1024,1024]{2,0,1:T(1,128)}) %all-gather.5.cloned.1.call-update) | async-done | bytes 4194320 | tf_op jit(solution)/shard_map/all_gather | solution.py:133
  63.8 5.1 copy.418
  70.3 11.0 %conditional.2 = (f32[1024,1024]{1,0:T(8,128)}) conditional(s32[]{:T(128)} %convert_element_type.169, () %tuple.29, f32[1024,1024]{1,0:T(8,128)} %bitcast.673), branch_computations={%region_2.3_spmd, %region_3.8_spmd} | conditional | flops 1619903488 | bytes 81994304 | solution.py:151
  81.3 2.8 broadcast_select_fusion.1
  84.1 72.3 %all-reduce.17.cloned.1.call-done = (bf16[2,192,1024]{2,1,0:T(8,128)(2,1)}, bf16[2,192,1024]{2,1,0:T(8,128)(2,1)}) async-done(((bf16[2,192,1024]{2,1,0:T(8,128)(2,1)}, bf16[2,192,1024]{2,1,0:T(8,128)(2,1)}), (bf16[2,192,1024]{2,1,0:T(8,128)(2,1)}, bf16[2,192,1024]{2,1,0:T(8,128)(2,1)})) %all-reduce.17.cloned.1.call-update) | async-done | bytes 1572880 | tf_op jit(solution)/shard_map/psum | solution.py:15
  158.6 5.9 pad_maximum_fusion
  166.5 218.3 %all-reduce.11.cloned.1.call-done = f32[1408,1024]{1,0:T(8,128)} async-done(((f32[1408,1024]{1,0:T(8,128)}), f32[1408,1024]{1,0:T(8,128)}) %all-reduce.11.cloned.1.call-update) | async-done | bytes 5767184 | tf_op jit(solution)/shard_map/psum | solution.py:157
  384.8 3.2 convert.64
  426.4 10.8 %all-reduce.15.cloned.1.call-start = ((), (), s32[]{:S(2)}) async-start(), calls=%async_computation.4 | async-start | bytes 3145728 | tf_op jit(solution)/shard_map/psum | solution.py:15
  456.5 24.9 %custom-call.116 = f32[2,1,128,128]{3,2,1,0:T(8,128)} custom-call(f32[2,1,128,128]{3,2,1,0:T(8,128)} %slice.761), custom_call_target="Cholesky" | custom-call | tf_op jit(solution)/shard_map/cholesky/custom-call.0 | solution.py:60
  484.1 21.1 %custom-call.117 = f32[2,1,1,128,128]{3,4,2,1,0:T(8,128)} custom-call(f32[2,1,1,128,128]{4,3,2,1,0:T(8,128)} %fusion.253), custom_call_target="InvertDiagBlocksLowerTriangular" | custom-call | tf_op jit(solution)/shard_map/triangular_solve/custom-call.4 | solution.py:61
  510.3 13.1 %custom-call.118 = f32[2,1,64,64]{3,2,1,0:T(8,128)} custom-call(f32[2,1,64,64]{3,2,1,0:T(8,128)} %fusion.147), custom_call_target="Cholesky" | custom-call | tf_op jit(solution)/shard_map/cholesky/custom-call.2 | solution.py:67
  525.9 11.2 %custom-call.119 = f32[2,1,1,64,64]{3,4,2,1,0:T(8,128)} custom-call(f32[2,1,1,64,64]{4,3,2,1,0:T(8,128)} %fusion.287), custom_call_target="InvertDiagBlocksLowerTriangular" | custom-call | tf_op jit(solution)/shard_map/triangular_solve/custom-call.5 | solution.py:69
  545.7 3.8 bitcast_select_fusion.18
  549.6 14.0 %conditional.3 = (f32[1024,1024]{1,0:T(8,128)}) conditional(s32[]{:T(128)} %convert_element_type.189, () %tuple.31, f32[1024,1024]{1,0:T(8,128)} %bitcast.678), branch_computations={%region_12.19_spmd, %region_13.20_spmd} | conditional | flops 1619903488 | bytes 81994304 | solution.py:151
  563.6 2.8 broadcast_select_fusion
  566.4 69.9 %all-reduce.15.cloned.1.call-done = (bf16[2,192,1024]{2,1,0:T(8,128)(2,1)}, bf16[2,192,1024]{2,1,0:T(8,128)(2,1)}) async-done(((bf16[2,192,1024]{2,1,0:T(8,128)(2,1)}, bf16[2,192,1024]{2,1,0:T(8,128)(2,1)}), (bf16[2,192,1024]{2,1,0:T(8,128)(2,1)}, bf16[2,192,1024]{2,1,0:T(8,128)(2,1)})) %all-reduce.15.cloned.1.call-update) | async-done | bytes 1572880 | tf_op jit(solution)/shard_map/psum | solution.py:15
  638.5 5.9 pad_maximum_fusion.1
  649.7 218.1 %all-reduce.13.cloned.1.call-done = f32[1408,1024]{1,0:T(8,128)} async-done(((f32[1408,1024]{1,0:T(8,128)}), f32[1408,1024]{1,0:T(8,128)}) %all-reduce.13.cloned.1.call-update) | async-done | bytes 5767184 | tf_op jit(solution)/shard_map/psum | solution.py:157
  867.8 3.2 convert.74
  909.9 23.6 %custom-call.120 = f32[2,1,128,128]{3,2,1,0:T(8,128)S(1)} custom-call(f32[2,1,128,128]{3,2,1,0:T(8,128)S(1)} %slice.799), custom_call_target="Cholesky" | custom-call | tf_op jit(solution)/shard_map/cholesky/custom-call.0 | solution.py:60
  935.2 19.7 %custom-call.121 = f32[2,1,1,128,128]{3,4,2,1,0:T(8,128)S(1)} custom-call(f32[2,1,1,128,128]{4,3,2,1,0:T(8,128)S(1)} %fusion.247), custom_call_target="InvertDiagBlocksLowerTriangular" | custom-call | tf_op jit(solution)/shard_map/triangular_solve/custom-call.4 | solution.py:61
  963.2 13.1 %custom-call.122 = f32[2,1,64,64]{3,2,1,0:T(8,128)} custom-call(f32[2,1,64,64]{3,2,1,0:T(8,128)} %fusion.148), custom_call_target="Cholesky" | custom-call | tf_op jit(solution)/shard_map/cholesky/custom-call.2 | solution.py:67
  978.8 11.2 %custom-call.123 = f32[2,1,1,64,64]{3,4,2,1,0:T(8,128)} custom-call(f32[2,1,1,64,64]{4,3,2,1,0:T(8,128)} %fusion.265), custom_call_target="InvertDiagBlocksLowerTriangular" | custom-call | tf_op jit(solution)/shard_map/triangular_solve/custom-call.5 | solution.py:69
  (311 shorter events, 164.5 us)
Async XLA Ops:
  7.2 436.4 %copy-start = (bf16[192,1024]{1,0:T(8,128)(2,1)S(1)}, bf16[192,1024]{1,0:T(8,128)(2,1)}, u32[]{:S(2)}) copy-start(bf16[192,1024]{1,0:T(8,128)(2,1)} %param.21) | copy-start | bytes 1179652
  7.2 56.6 %all-gather.5.cloned.1.call-start = ((), (), s32[]{:S(2)}) async-start(), calls=%async_computation.2 | async-start | bytes 4456448 | tf_op jit(solution)/shard_map/all_gather | solution.py:133
  9.2 147.2 %all-reduce.17.cloned.1.call-start = ((), (), s32[]{:S(2)}) async-start(), calls=%async_computation.5 | async-start | bytes 3145728 | tf_op jit(solution)/shard_map/psum | solution.py:15
  11.6 57.3 %copy-start.34 = (pred[2,192]{1,0:T(4,128)(4,1)}, pred[2,192]{1,0:T(4,128)(4,1)S(1)}, u32[]{:S(2)}) copy-start(pred[2,192]{1,0:T(4,128)(4,1)S(1)} %compare_and_fusion) | copy-start | bytes 1156
  13.1 55.8 %copy-start.5 = (bf16[2,192,1024]{2,1,0:T(8,128)(2,1)}, bf16[2,192,1024]{2,1,0:T(8,128)(2,1)S(1)}, u32[]{:S(2)}) copy-start(bf16[2,192,1024]{2,1,0:T(8,128)(2,1)S(1)} %get-tuple-element.22) | copy-start | bytes 2359300
  70.2 314.6 %all-reduce.11.cloned.1.call-start = ((), (), s32[]{:S(2)}) async-start(), calls=%async_computation | async-start | bytes 11534336 | tf_op jit(solution)/shard_map/psum | solution.py:157
  164.6 381.1 %all-gather.7.cloned.1.call-start = ((), (), s32[]{:S(2)}) async-start(), calls=%async_computation.3 | async-start | bytes 4456448 | tf_op jit(solution)/shard_map/all_gather | solution.py:193
  166.4 257.5 %copy-start.35 = (pred[2]{0:T(512)(128)(4,1)}, pred[2]{0:T(512)(128)(4,1)S(1)}, u32[]{:S(2)}) copy-start(pred[2]{0:T(512)(128)(4,1)S(1)} %get-tuple-element.138) | copy-start | bytes 10
  166.5 221.6 %copy-start.25 = (bf16[2,192,1024]{2,1,0:T(8,128)(2,1)S(1)}, bf16[2,192,1024]{2,1,0:T(8,128)(2,1)}, u32[]{:S(2)}) copy-start(bf16[2,192,1024]{2,1,0:T(8,128)(2,1)} %get-tuple-element.48) | copy-start | bytes 2359300
  400.9 13.6 %slice-start.3 = ((s8[5767168]{0:T(1024)(128)(4,1)}), s8[1572864]{0:T(1024)(128)(4,1)S(1)}, s32[]{:S(2)}) async-start(s8[5767168]{0:T(1024)(128)(4,1)} %bitcast.676), calls=%async_computation.9 | async-start | bytes 3145728
  423.8 19.8 %copy-start.6 = (bf16[2,192,1024]{2,1,0:T(8,128)(2,1)S(1)}, bf16[2,192,1024]{2,1,0:T(8,128)(2,1)}, u32[]{:S(2)}) copy-start(bf16[2,192,1024]{2,1,0:T(8,128)(2,1)} %copy-done.5) | copy-start | bytes 2359300
  425.6 23.4 %copy-start.16 = (f32[2,64,1024]{2,1,0:T(8,128)}, f32[2,64,1024]{2,1,0:T(8,128)S(1)}, u32[]{:S(2)}) copy-start(f32[2,64,1024]{2,1,0:T(8,128)S(1)} %fusion.133) | copy-start | bytes 1572868
  425.6 21.6 %copy-start.36 = (pred[2]{0:T(512)(128)(4,1)S(1)}, pred[2]{0:T(512)(128)(4,1)}, u32[]{:S(2)}) copy-start(pred[2]{0:T(512)(128)(4,1)} %copy-done.35) | copy-start | bytes 10
  426.4 209.9 %all-reduce.15.cloned.1.call-start = ((), (), s32[]{:S(2)}) async-start(), calls=%async_computation.4 | async-start | bytes 3145728 | tf_op jit(solution)/shard_map/psum | solution.py:15
  549.5 97.2 %copy-start.20 = (bf16[2,1,192,1024]{3,2,0,1:T(8,128)(2,1)}, bf16[2,1,192,1024]{3,2,0,1:T(8,128)(2,1)S(1)}, u32[]{:S(2)}) copy-start(bf16[2,1,192,1024]{3,2,0,1:T(8,128)(2,1)S(1)} %get-tuple-element.52) | copy-start | bytes 2359300
  549.5 318.3 %all-reduce.13.cloned.1.call-start = ((), (), s32[]{:S(2)}) async-start(), calls=%async_computation.1 | async-start | bytes 11534336 | tf_op jit(solution)/shard_map/psum | solution.py:157
  649.7 221.4 %copy-start.26 = (bf16[2,192,1024]{2,1,0:T(8,128)(2,1)S(1)}, bf16[2,192,1024]{2,1,0:T(8,128)(2,1)}, u32[]{:S(2)}) copy-start(bf16[2,192,1024]{2,1,0:T(8,128)(2,1)} %get-tuple-element.46) | copy-start | bytes 2359300
  884.5 13.8 %slice-start = ((s8[5767168]{0:T(1024)(128)(4,1)}), s8[1572864]{0:T(1024)(128)(4,1)S(1)}, s32[]{:S(2)}) async-start(s8[5767168]{0:T(1024)(128)(4,1)} %bitcast.674), calls=%async_computation.6 | async-start | bytes 3145728
  962.4 36.0 %copy-start.13 = (bf16[2,192,1024]{2,1,0:T(8,128)(2,1)S(1)}, bf16[2,192,1024]{2,1,0:T(8,128)(2,1)}, u32[]{:S(2)}) copy-start(bf16[2,192,1024]{2,1,0:T(8,128)(2,1)} %get-tuple-element.45) | copy-start | bytes 2359300
  962.4 36.0 %copy-start.40 = (pred[2]{0:T(512)(128)(4,1)S(1)}, pred[2]{0:T(512)(128)(4,1)}, u32[]{:S(2)}) copy-start(pred[2]{0:T(512)(128)(4,1)} %broadcast_compare_fusion.1) | copy-start | bytes 10
  962.4 36.0 %copy-start.41 = (pred[2]{0:T(512)(128)(4,1)S(1)}, pred[2]{0:T(512)(128)(4,1)}, u32[]{:S(2)}) copy-start(pred[2]{0:T(512)(128)(4,1)} %get-tuple-element.49) | copy-start | bytes 10
  992.5 7.5 copy-start.21
  992.6 7.5 copy-start.32
  992.6 7.5 copy-start.48
  (45 other events, 137.5 us)
Sparse Core Ops, SparseCore 0:
  10.7 53.0 all-gather.4
  70.3 86.0 all-reduce.16
  164.7 220.1 all-reduce.10
  426.5 51.9 all-gather.6
  549.7 86.5 all-reduce.14
  644.6 223.1 all-reduce.12

commit v9 on v7

--- a/solution.py
+++ b/solution.py
@@ -79,12 +79,16 @@
     count = order // width
     lead = raw_factors.shape[:-1]
     rest = raw_factors.reshape(-1, order).astype(jnp.float32)
+    blocks = jnp.stack([packed[s * width:(s + 1) * width, s * width:(s + 1) * width] for s in range(count)])
+    eye = jnp.eye(width, dtype=jnp.bool_)
+    lower = jnp.arange(width)[:, None] > jnp.arange(width)[None, :]
+    inverses = jnp.where(lower, jnp.swapaxes(blocks, -1, -2), 0.0) + jnp.where(
+        eye, 1.0 / jnp.where(eye, blocks, 1.0), 0.0
+    )
     done = []
     for step in range(count):
         lo, hi = step * width, (step + 1) * width
-        block = packed[lo:hi, lo:hi]
-        inverse = jnp.tril(block.T, -1) + jnp.diag(1.0 / jnp.diagonal(block))
-        part = jnp.dot(rest[:, :width], inverse.T, precision=fine)
+        part = jnp.dot(rest[:, :width], inverses[step].T, precision=fine)
         done.append(part)
         if step < count - 1:
             rest = rest[:, width:] - jnp.dot(part, packed[hi:, lo:hi].T, precision=fine)

time: 1010 us -> 1000 us (0.990)
    gather x16 -> x0, local copies, waits for them, and re-layouts: 25.4 us -> none  [solve_packed(): inverse = jnp.tril(block.T, -1) + jnp.diag(1.0 / jnp.diagonal(block))]
    unnamed x124 -> x135, local copies, waits for them, and re-layouts: 10.4 us -> 24.6 us
where the time goes in v9:
time: 1000 us; the launch traced here: 995 us
  waiting for transfers between devices  633 us (63%)
  other arithmetic  206 us (21%)
  matrix products  72.2 us (7%)
  local copies, waits for them, and re-layouts  52.5 us (5%)
  loops' own time  15.7 us (2%)
  between operations  15.6 us (2%)
    psum x2, waiting for transfers between devices, on_device(): lax.psum(jnp.concatenate([own_chol, relay.reshape(-1, tile_order)], axis=...  436 us
    psum x2, waiting for transfers between devices, broadcast(): return lax.psum(jnp.where(mine, shard, jnp.zeros_like(shard)), axis)  147 us
    another operation x7, other arithmetic, factor_inverse(): lax.linalg.cholesky(gram[..., :width, :width], symmetrize_input=False)  52.7 us
    all_gather x1, waiting for transfers between devices, on_device(): whole_tile = lax.all_gather(diagonal[diag_slot], 'col', axis=0, tiled=True)  50.1 us
    another operation x5, other arithmetic, factor_inverse(): lax.linalg.triangular_solve(head, eye, left_side=True, lower=True)  46.1 us
    another operation x7, other arithmetic, factor_inverse(): tail = jnp.tril(lax.linalg.cholesky(tail, symmetrize_input=False))  28.7 us
    another operation x5, other arithmetic, factor_inverse(): lax.linalg.triangular_solve(tail, eye_rest, left_side=True, lower=True)  26.5 us
    unnamed x135, local copies, waits for them, and re-layouts  24.6 us
  transfers between devices with their start and end apart: 6, of which 5 were waited for; matrix products, arithmetic and copies ran while one was open for 13% of the time, Pallas kernels for 0%

profile of v9, /device:TPU:37, one launch (start us, length us, event | category | flops | bytes accessed | tf_op | source)
XLA Modules:
  0.0 995.5 jit_solution(384152391572161389)
XLA Ops:
  13.7 50.1 %all-gather.5.cloned.1.call-done = f32[1,1024,1024]{2,0,1:T(1,128)} async-done(((f32[1,64,1024]{2,0,1:T(1,128)}), f32[1,1024,1024]{2,0,1:T(1,128)}) %all-gather.5.cloned.1.call-update) | async-done | bytes 4194320 | tf_op jit(solution)/shard_map/all_gather | solution.py:137
  63.8 5.1 copy.503
  70.3 9.8 conditional.2
  70.3 2.5 broadcast.401
  80.1 2.8 broadcast_select_fusion.1
  82.8 73.7 %all-reduce.17.cloned.1.call-done = (bf16[2,192,1024]{2,1,0:T(8,128)(2,1)}, bf16[2,192,1024]{2,1,0:T(8,128)(2,1)}) async-done(((bf16[2,192,1024]{2,1,0:T(8,128)(2,1)}, bf16[2,192,1024]{2,1,0:T(8,128)(2,1)}), (bf16[2,192,1024]{2,1,0:T(8,128)(2,1)}, bf16[2,192,1024]{2,1,0:T(8,128)(2,1)})) %all-reduce.17.cloned.1.call-update) | async-done | bytes 1572880 | tf_op jit(solution)/shard_map/psum | solution.py:15
  158.7 5.7 pad_maximum_fusion
  167.7 218.2 %all-reduce.11.cloned.1.call-done = f32[1408,1024]{1,0:T(8,128)} async-done(((f32[1408,1024]{1,0:T(8,128)}), f32[1408,1024]{1,0:T(8,128)}) %all-reduce.11.cloned.1.call-update) | async-done | bytes 5767184 | tf_op jit(solution)/shard_map/psum | solution.py:161
  385.8 3.2 convert.64
  445.0 24.9 %custom-call.84 = f32[2,1,128,128]{3,2,1,0:T(8,128)} custom-call(f32[2,1,128,128]{3,2,1,0:T(8,128)} %slice.801), custom_call_target="Cholesky" | custom-call | tf_op jit(solution)/shard_map/cholesky/custom-call.0 | solution.py:60
  472.6 21.1 %custom-call.85 = f32[2,1,1,128,128]{3,4,2,1,0:T(8,128)} custom-call(f32[2,1,1,128,128]{4,3,2,1,0:T(8,128)} %fusion.255), custom_call_target="InvertDiagBlocksLowerTriangular" | custom-call | tf_op jit(solution)/shard_map/triangular_solve/custom-call.4 | solution.py:61
  498.9 13.1 %custom-call.86 = f32[2,1,64,64]{3,2,1,0:T(8,128)} custom-call(f32[2,1,64,64]{3,2,1,0:T(8,128)} %fusion.147), custom_call_target="Cholesky" | custom-call | tf_op jit(solution)/shard_map/cholesky/custom-call.2 | solution.py:67
  514.5 11.4 %custom-call.87 = f32[2,1,1,64,64]{3,4,2,1,0:T(8,128)} custom-call(f32[2,1,1,64,64]{4,3,2,1,0:T(8,128)} %fusion.273), custom_call_target="InvertDiagBlocksLowerTriangular" | custom-call | tf_op jit(solution)/shard_map/triangular_solve/custom-call.5 | solution.py:69
  535.6 3.5 bitcast_select_fusion.18
  539.2 10.9 %conditional.3 = (f32[1024,1024]{1,0:T(8,128)}) conditional(s32[]{:T(128)} %convert_element_type.189, () %tuple.31, f32[1024,1024]{1,0:T(8,128)} %bitcast.698), branch_computations={%region_12.19_spmd, %region_13.20_spmd} | conditional | flops 1619903488 | bytes 81994304 | solution.py:155
  550.1 2.8 broadcast_select_fusion
  552.9 72.9 %all-reduce.15.cloned.1.call-done = (bf16[2,192,1024]{2,1,0:T(8,128)(2,1)}, bf16[2,192,1024]{2,1,0:T(8,128)(2,1)}) async-done(((bf16[2,192,1024]{2,1,0:T(8,128)(2,1)}, bf16[2,192,1024]{2,1,0:T(8,128)(2,1)}), (bf16[2,192,1024]{2,1,0:T(8,128)(2,1)}, bf16[2,192,1024]{2,1,0:T(8,128)(2,1)})) %all-reduce.15.cloned.1.call-update) | async-done | bytes 1572880 | tf_op jit(solution)/shard_map/psum | solution.py:15
  628.1 5.7 pad_maximum_fusion.1
  638.0 218.0 %all-reduce.13.cloned.1.call-done = f32[1408,1024]{1,0:T(8,128)} async-done(((f32[1408,1024]{1,0:T(8,128)}), f32[1408,1024]{1,0:T(8,128)}) %all-reduce.13.cloned.1.call-update) | async-done | bytes 5767184 | tf_op jit(solution)/shard_map/psum | solution.py:161
  856.0 3.2 convert.74
  888.0 25.1 %custom-call.88 = f32[2,1,128,128]{3,2,1,0:T(8,128)} custom-call(f32[2,1,128,128]{3,2,1,0:T(8,128)} %slice.847), custom_call_target="Cholesky" | custom-call | tf_op jit(solution)/shard_map/cholesky/custom-call.0 | solution.py:60
  915.8 21.1 %custom-call.89 = f32[2,1,1,128,128]{3,4,2,1,0:T(8,128)} custom-call(f32[2,1,1,128,128]{4,3,2,1,0:T(8,128)} %fusion.249), custom_call_target="InvertDiagBlocksLowerTriangular" | custom-call | tf_op jit(solution)/shard_map/triangular_solve/custom-call.4 | solution.py:61
  947.1 13.1 %custom-call.90 = f32[2,1,64,64]{3,2,1,0:T(8,128)} custom-call(f32[2,1,64,64]{3,2,1,0:T(8,128)} %fusion.148), custom_call_target="Cholesky" | custom-call | tf_op jit(solution)/shard_map/cholesky/custom-call.2 | solution.py:67
  962.8 11.4 %custom-call.91 = f32[2,1,1,64,64]{3,4,2,1,0:T(8,128)} custom-call(f32[2,1,1,64,64]{4,3,2,1,0:T(8,128)} %fusion.267), custom_call_target="InvertDiagBlocksLowerTriangular" | custom-call | tf_op jit(solution)/shard_map/triangular_solve/custom-call.5 | solution.py:69
  (295 shorter events, 155.6 us)
Async XLA Ops:
  7.2 424.6 %copy-start = (bf16[192,1024]{1,0:T(8,128)(2,1)S(1)}, bf16[192,1024]{1,0:T(8,128)(2,1)}, u32[]{:S(2)}) copy-start(bf16[192,1024]{1,0:T(8,128)(2,1)} %param.21) | copy-start | bytes 1179652
  7.2 56.6 %all-gather.5.cloned.1.call-start = ((), (), s32[]{:S(2)}) async-start(), calls=%async_computation.2 | async-start | bytes 4456448 | tf_op jit(solution)/shard_map/all_gather | solution.py:137
  9.2 147.3 %all-reduce.17.cloned.1.call-start = ((), (), s32[]{:S(2)}) async-start(), calls=%async_computation.5 | async-start | bytes 3145728 | tf_op jit(solution)/shard_map/psum | solution.py:15
  70.2 315.6 %all-reduce.11.cloned.1.call-start = ((), (), s32[]{:S(2)}) async-start(), calls=%async_computation | async-start | bytes 11534336 | tf_op jit(solution)/shard_map/psum | solution.py:161
  164.5 371.1 %all-gather.7.cloned.1.call-start = ((), (), s32[]{:S(2)}) async-start(), calls=%async_computation.3 | async-start | bytes 4456448 | tf_op jit(solution)/shard_map/all_gather | solution.py:197
  167.7 221.5 %copy-start.24 = (bf16[2,192,1024]{2,1,0:T(8,128)(2,1)S(1)}, bf16[2,192,1024]{2,1,0:T(8,128)(2,1)}, u32[]{:S(2)}) copy-start(bf16[2,192,1024]{2,1,0:T(8,128)(2,1)} %get-tuple-element.48) | copy-start | bytes 2359300
  405.5 7.6 slice-start
  423.7 13.5 %copy-start.15 = (f32[2,64,1024]{2,1,0:T(8,128)}, f32[2,64,1024]{2,1,0:T(8,128)S(1)}, u32[]{:S(2)}) copy-start(f32[2,64,1024]{2,1,0:T(8,128)S(1)} %fusion.133) | copy-start | bytes 1572868
  423.7 11.7 %copy-start.41 = (pred[2]{0:T(512)(128)(4,1)S(1)}, pred[2]{0:T(512)(128)(4,1)}, u32[]{:S(2)}) copy-start(pred[2]{0:T(512)(128)(4,1)} %copy-done.39) | copy-start | bytes 10
  424.6 201.3 %all-reduce.15.cloned.1.call-start = ((), (), s32[]{:S(2)}) async-start(), calls=%async_computation.4 | async-start | bytes 3145728 | tf_op jit(solution)/shard_map/psum | solution.py:15
  434.0 5.3 copy-start.43
  539.1 96.4 %copy-start.19 = (bf16[2,1,192,1024]{3,2,0,1:T(8,128)(2,1)}, bf16[2,1,192,1024]{3,2,0,1:T(8,128)(2,1)S(1)}, u32[]{:S(2)}) copy-start(bf16[2,1,192,1024]{3,2,0,1:T(8,128)(2,1)S(1)} %get-tuple-element.52) | copy-start | bytes 2359300
  539.1 316.8 %all-reduce.13.cloned.1.call-start = ((), (), s32[]{:S(2)}) async-start(), calls=%async_computation.1 | async-start | bytes 11534336 | tf_op jit(solution)/shard_map/psum | solution.py:161
  637.9 222.9 %copy-start.25 = (bf16[2,192,1024]{2,1,0:T(8,128)(2,1)S(1)}, bf16[2,192,1024]{2,1,0:T(8,128)(2,1)}, u32[]{:S(2)}) copy-start(bf16[2,192,1024]{2,1,0:T(8,128)(2,1)} %get-tuple-element.46) | copy-start | bytes 2359300
  856.0 6.1 copy-start.4
  863.2 5.4 copy-start.5
  878.2 36.0 %copy-start.35 = (pred[128,128]{1,0:T(8,128)(4,1)S(1)}, pred[128,128]{1,0:T(8,128)(4,1)}, u32[]{:S(2)}) copy-start(pred[128,128]{1,0:T(8,128)(4,1)} %iota_compare_fusion.25) | copy-start | bytes 49156
  944.2 16.0 %copy-start.37 = (pred[64,64]{1,0:T(8,128)(4,1)S(1)}, pred[64,64]{1,0:T(8,128)(4,1)}, u32[]{:S(2)}) copy-start(pred[64,64]{1,0:T(8,128)(4,1)} %iota_compare_fusion.30) | copy-start | bytes 12292
  944.2 17.0 %copy-start.36 = (pred[64,64]{1,0:T(8,128)(4,1)S(1)}, pred[64,64]{1,0:T(8,128)(4,1)}, u32[]{:S(2)}) copy-start(pred[64,64]{1,0:T(8,128)(4,1)} %iota_compare_fusion.29) | copy-start | bytes 12292
  961.1 22.5 %copy-start.46 = (pred[2]{0:T(512)(128)(4,1)S(1)}, pred[2]{0:T(512)(128)(4,1)}, u32[]{:S(2)}) copy-start(pred[2]{0:T(512)(128)(4,1)} %copy-done.44) | copy-start | bytes 10
  961.1 22.5 %copy-start.49 = (pred[2]{0:T(512)(128)(4,1)S(1)}, pred[2]{0:T(512)(128)(4,1)}, u32[]{:S(2)}) copy-start(pred[2]{0:T(512)(128)(4,1)} %get-tuple-element.49) | copy-start | bytes 10
  962.8 20.8 %copy-start.56 = (pred[2]{0:T(512)(128)(4,1)S(1)}, pred[2]{0:T(512)(128)(4,1)}, u32[]{:S(2)}) copy-start(pred[2]{0:T(512)(128)(4,1)} %broadcast_and_fusion) | copy-start | bytes 10
  977.0 7.6 copy-start.20
  977.0 7.6 copy-start.32
  (39 other events, 101.8 us)
Sparse Core Ops, SparseCore 0:
  10.7 53.0 all-gather.4
  70.3 86.1 all-reduce.16
  164.6 221.1 all-reduce.10
  424.7 51.8 all-gather.6
  539.3 86.5 all-reduce.14
  633.9 221.9 all-reduce.12
